TPU v7x, 512 devices: a whole 4x4x16 slice. The times are simulated.
512 devices in a mesh: bulk: 32 (over z, core), seg: 16 (over y, x).
Axes of the slice: x: 4, y: 4, z: 16, core: 2. Of those that a mesh axis runs over, the one named last changes fastest.
Arguments:
- em_cutouts: bfloat16 [32, 16, 40, 4096], P('bulk', 'seg'), may hold values from -6 to 6
- mask_cutouts: bfloat16 [32, 16, 40, 2, 4096], P('bulk', 'seg'), may hold values from 0 to 1
- live_count: int32 [32, 16], replicated, may hold values from 1 to 40, as said below
- segment_ids: int32 [32, 16, 40], P('bulk', 'seg'), may hold values from 0 to 127
- patch_weight: bfloat16 [32, 24], replicated, may hold values from -1.75 to 1.75
- conv_weight: bfloat16 [3, 27, 32, 32], replicated, may hold values from -0.3125 to 0.3125
- conv_bias: float32 [4, 32], replicated, may hold values from -3 to 3
- score_weight: float32 [32], replicated, may hold values from -2 to 2
- embed_weight: bfloat16 [32, 128], replicated, may hold values from -1 to 1
Outputs:
- pair_score: bfloat16 [32, 16, 40], P('bulk', 'seg')
- segment_embed: float32 [4096, 128], P(('bulk', 'seg'))
Inputs may be any that keep to these rules, and one draw needn't show every extreme that they name: `live_count`: along bulk, the 32 devices of each seg column hold 320 live slots in all, and one device of every column holds 40; so every owner scores exactly 10 pairs and gets at most 2 from any one device.
All inputs are finite; a program needn't handle non-finite values.
Results may differ from a plain program's by a relative error of at most 0.012.
Values may be sent and summed in bfloat16 or wider, within the bound.
No kernel may reach another device: no remote copies, remote signals or barrier semaphores. Data moves between devices by JAX's collectives and lax.ppermute only.
A program may use at most 192 MiB of HBM per device.

v0:
```python
import jax
import jax.numpy as jnp
from jax import lax
from jax.sharding import PartitionSpec as P
from jax.experimental import pallas as pl
from jax.experimental.pallas import tpu as pltpu

CS = 16
LAYERS = 3
SEG_DEV = 8
BLOCK_PAIRS = 8
PAD_ROWS = 16


def conv_kernel(h_ref, w_ref, b_ref, o_ref, pad_ref, col_ref):
    rows, lanes = h_ref.shape
    side = CS // 2
    edge = PAD_ROWS
    pad_ref[0:edge, :] = jnp.zeros((edge, lanes), jnp.float32)
    pad_ref[edge + rows:, :] = jnp.zeros((edge, lanes), jnp.float32)
    pad_ref[edge:edge + rows, :] = h_ref[...].astype(jnp.float32)
    row_id = lax.broadcasted_iota(jnp.int32, (rows, lanes), 0)
    y_pos = row_id % side
    x_pos = (row_id // side) % side
    for layer_index in range(LAYERS):
        for shift_a in range(3):
            for shift_b in range(3):
                tap = shift_a * 3 + shift_b
                offset = (shift_a - 1) * side + (shift_b - 1)
                window = pad_ref[edge + offset:edge + offset + rows, :]
                x_to = x_pos + (shift_a - 1)
                y_to = y_pos + (shift_b - 1)
                inside = (x_to >= 0) & (x_to < side) & (y_to >= 0) & (y_to < side)
                col_ref[:, tap * lanes:(tap + 1) * lanes] = jnp.where(
                    inside, window, 0.0
                ).astype(jnp.bfloat16)
        summed = jnp.dot(col_ref[...], w_ref[layer_index], preferred_element_type=jnp.float32)
        hidden = jnp.maximum(summed + b_ref[layer_index], 0.0).astype(jnp.bfloat16)
        if layer_index + 1 < LAYERS:
            pad_ref[edge:edge + rows, :] = hidden.astype(jnp.float32)
        else:
            o_ref[...] = hidden


def conv_layers(volume, conv_weight, conv_bias):
    total_rows, lanes = volume.shape
    side = CS // 2
    channels = conv_weight.shape[2]
    taps = conv_weight.reshape(LAYERS, 3, 3, 3, channels, channels).transpose(0, 1, 2, 3, 5, 4)
    z_in = jnp.arange(side)[:, None, None, None]
    z_out = jnp.arange(side)[None, None, :, None]
    band = jnp.zeros((LAYERS, 3, 3, side, channels, side, channels), jnp.bfloat16)
    for shift_c in range(3):
        hit = z_in - z_out + 1 == shift_c
        band = band + jnp.where(hit, taps[:, :, :, shift_c][:, :, :, None, :, None, :], 0)
    band = band.reshape(LAYERS, 9 * lanes, lanes)
    bias = jnp.tile(conv_bias[1:], (1, side)).reshape(LAYERS, 1, lanes)
    block_rows = BLOCK_PAIRS * side * side
    return pl.pallas_call(
        conv_kernel,
        grid=(total_rows // block_rows,),
        in_specs=[
            pl.BlockSpec((block_rows, lanes), lambda i: (i, 0)),
            pl.BlockSpec((LAYERS, 9 * lanes, lanes), lambda i: (0, 0, 0)),
            pl.BlockSpec((LAYERS, 1, lanes), lambda i: (0, 0, 0)),
        ],
        out_specs=pl.BlockSpec((block_rows, lanes), lambda i: (i, 0)),
        out_shape=jax.ShapeDtypeStruct((total_rows, lanes), jnp.bfloat16),
        scratch_shapes=[
            pltpu.VMEM((block_rows + 2 * PAD_ROWS, lanes), jnp.float32),
            pltpu.VMEM((block_rows, 9 * lanes), jnp.bfloat16),
        ],
    )(volume, band, bias)


def run_network(
    em_rows, mask_rows, patch_weight, conv_weight, conv_bias, score_weight, embed_weight
):
    rows_here = em_rows.shape[0]
    side_half = CS // 2
    voxel_count = side_half * side_half * side_half
    channels = conv_weight.shape[2]
    lanes = side_half * channels
    highest = lax.Precision.HIGHEST
    stacked = jnp.concatenate([em_rows[:, None, :], mask_rows], axis=1)
    volume_in = stacked.reshape(rows_here, 3, CS, CS, CS)
    patch_kernel = patch_weight.reshape(channels, 3, 2, 2, 2)
    first_out = lax.conv_general_dilated(
        volume_in,
        patch_kernel,
        (2, 2, 2),
        "VALID",
        dimension_numbers=("NCDHW", "OIDHW", "NDHWC"),
        preferred_element_type=jnp.float32,
    )
    volume = jax.nn.relu(first_out + conv_bias[0]).astype(jnp.bfloat16)
    volume = volume.reshape(rows_here * side_half * side_half, lanes)
    hidden = conv_layers(volume, conv_weight, conv_bias)
    hidden = hidden.reshape(rows_here, side_half * side_half, side_half, channels)
    intersection = mask_rows[:, 0].astype(jnp.float32) * mask_rows[:, 1].astype(jnp.float32)
    intersection = intersection.reshape(rows_here, side_half, 2, side_half, 2, side_half, 2)
    boundary = jnp.mean(intersection, axis=(2, 4, 6))
    boundary = boundary.reshape(rows_here, side_half * side_half, side_half) + 0.1
    pooled = jnp.sum(hidden.astype(jnp.float32) * boundary[..., None], axis=(1, 2))
    pooled = pooled / jnp.sum(boundary, axis=(1, 2))[:, None]
    logits = jnp.dot(pooled, score_weight, precision=highest)
    scores = jax.nn.sigmoid(logits).astype(jnp.bfloat16)
    embedded = jnp.tanh(jnp.dot(pooled, embed_weight.astype(jnp.float32), precision=highest))
    contrib = (scores.astype(jnp.float32)[:, None] * embedded).astype(jnp.bfloat16)
    return (scores, contrib)


def per_device(
    em_cutouts,
    mask_cutouts,
    live_count,
    segment_ids,
    patch_weight,
    conv_weight,
    conv_bias,
    score_weight,
    embed_weight,
):
    bulk_index = lax.axis_index("bulk")
    seg_index = lax.axis_index("seg")
    slots = em_cutouts.shape[2]
    em_local = em_cutouts.reshape(slots, -1)
    mask_local = mask_cutouts.reshape(slots, 2, -1)
    own_count = live_count[bulk_index, seg_index]
    slot_ids = jnp.arange(slots, dtype=jnp.int32)
    live_slot = slot_ids < own_count
    part_score, part_contrib = run_network(
        em_local, mask_local, patch_weight, conv_weight, conv_bias, score_weight, embed_weight
    )
    scores = jnp.where(live_slot, part_score, 0)
    contribs = jnp.where(live_slot[:, None], part_contrib, 0)
    seg_local = jnp.where(live_slot, segment_ids.reshape(slots), -1)
    packed = jnp.concatenate([contribs, seg_local[:, None].astype(jnp.bfloat16)], axis=1)
    gathered = lax.all_gather(packed, "seg", tiled=True)
    all_contrib = gathered[:, :-1]
    all_ids = gathered[:, -1].astype(jnp.int32)
    wanted = seg_index * SEG_DEV + jnp.arange(SEG_DEV, dtype=jnp.int32)
    onehot = (all_ids[None, :] == wanted[:, None]).astype(jnp.bfloat16)
    summed = jnp.dot(onehot, all_contrib, preferred_element_type=jnp.float32)
    return (scores.reshape(1, 1, slots), summed)


def solution(mesh):
    in_specs = (
        P("bulk", "seg", None, None),
        P("bulk", "seg", None, None, None),
        P(),
        P("bulk", "seg", None),
        P(),
        P(),
        P(),
        P(),
        P(),
    )
    out_specs = (P("bulk", "seg", None), P(("bulk", "seg"), None))
    return jax.shard_map(
        per_device, mesh=mesh, in_specs=in_specs, out_specs=out_specs, check_vma=False
    )
```

profile of v0, /device:TPU:2, one launch (start us, length us, event | category | flops | bytes accessed | tf_op | source)
XLA Modules:
  0.0 218.8 jit_solution(12982271277168323156)
XLA Ops:
  2.0 2.0 slice_bitcast_fusion.2
  4.1 8.5 %broadcast_in_dim.99 = bf16[3,3,3,8,32,8,32]{6,5,4,3,2,1,0:T(8,128)(2,1)} broadcast(bf16[3,3,3,32,32]{4,3,2,1,0:T(8,128)(2,1)S(1)} %copy.47), dimensions={0,1,2,4,6} | broadcast | bytes 3594240 | tf_op jit(solution)/shard_map/jit(_where)/broadcast_in_dim | solution.py:55
  12.7 16.1 %broadcast_in_dim.100 = bf16[3,2304,256]{2,1,0:T(8,128)(2,1)S(1)} reshape(bf16[3,3,3,8,32,8,32]{6,5,4,3,2,1,0:T(8,128)(2,1)} %broadcast_in_dim.99) | data formatting | bytes 7077888 | tf_op jit(solution)/shard_map/jit(_where)/broadcast_in_dim | solution.py:55
  28.8 1.8 copy.48
  30.5 9.5 %broadcast_in_dim.106 = bf16[3,3,3,8,32,8,32]{6,5,4,3,2,1,0:T(8,128)(2,1)} broadcast(bf16[3,3,3,32,32]{4,3,2,1,0:T(8,128)(2,1)} %copy.48), dimensions={0,1,2,4,6} | broadcast | bytes 3594240 | tf_op jit(solution)/shard_map/jit(_where)/broadcast_in_dim | solution.py:55
  40.0 17.4 %broadcast_in_dim.107 = bf16[3,2304,256]{2,1,0:T(8,128)(2,1)} reshape(bf16[3,3,3,8,32,8,32]{6,5,4,3,2,1,0:T(8,128)(2,1)} %broadcast_in_dim.106) | data formatting | bytes 7077888 | tf_op jit(solution)/shard_map/jit(_where)/broadcast_in_dim | solution.py:55
  59.2 9.5 %broadcast_in_dim.112 = bf16[3,3,3,8,32,8,32]{6,5,4,3,2,1,0:T(8,128)(2,1)} broadcast(bf16[3,3,3,32,32]{4,3,2,1,0:T(8,128)(2,1)} %copy.49), dimensions={0,1,2,4,6} | broadcast | bytes 3594240 | tf_op jit(solution)/shard_map/jit(_where)/broadcast_in_dim | solution.py:55
  68.7 17.4 %broadcast_in_dim.113 = bf16[3,2304,256]{2,1,0:T(8,128)(2,1)} reshape(bf16[3,3,3,8,32,8,32]{6,5,4,3,2,1,0:T(8,128)(2,1)} %broadcast_in_dim.112) | data formatting | bytes 7077888 | tf_op jit(solution)/shard_map/jit(_where)/broadcast_in_dim | solution.py:55
  86.1 2.4 %broadcast_in_dim.102 = pred[3,3,8,32,8,32]{5,4,3,2,1,0:T(8,128)(4,1)} broadcast(pred[8,8]{1,0:T(8,128)(4,1)S(1)} %fusion.21), dimensions={2,4} | broadcast | bytes 589888 | tf_op jit(solution)/shard_map/jit(_where)/broadcast_in_dim | solution.py:55
  88.5 6.1 %broadcast_in_dim.103 = pred[2304,256]{1,0:T(8,128)(4,1)} reshape(pred[3,3,8,32,8,32]{5,4,3,2,1,0:T(8,128)(4,1)} %broadcast_in_dim.102) | data formatting | bytes 1179648 | tf_op jit(solution)/shard_map/jit(_where)/broadcast_in_dim | solution.py:55
  94.6 2.4 %broadcast_in_dim.108 = pred[3,3,8,32,8,32]{5,4,3,2,1,0:T(8,128)(4,1)} broadcast(pred[8,8]{1,0:T(8,128)(4,1)S(1)} %fusion.20), dimensions={2,4} | broadcast | bytes 589888 | tf_op jit(solution)/shard_map/jit(_where)/broadcast_in_dim | solution.py:55
  97.1 6.1 %broadcast_in_dim.109 = pred[2304,256]{1,0:T(8,128)(4,1)} reshape(pred[3,3,8,32,8,32]{5,4,3,2,1,0:T(8,128)(4,1)} %broadcast_in_dim.108) | data formatting | bytes 1179648 | tf_op jit(solution)/shard_map/jit(_where)/broadcast_in_dim | solution.py:55
  103.1 2.4 %broadcast_in_dim.95 = pred[3,3,8,32,8,32]{5,4,3,2,1,0:T(8,128)(4,1)} broadcast(pred[8,8]{1,0:T(8,128)(4,1)S(1)} %fusion.22), dimensions={2,4} | broadcast | bytes 589888 | tf_op jit(solution)/shard_map/jit(_where)/broadcast_in_dim | solution.py:55
  105.6 6.1 %broadcast_in_dim.96 = pred[2304,256]{1,0:T(8,128)(4,1)} reshape(pred[3,3,8,32,8,32]{5,4,3,2,1,0:T(8,128)(4,1)} %broadcast_in_dim.95) | data formatting | bytes 1179648 | tf_op jit(solution)/shard_map/jit(_where)/broadcast_in_dim | solution.py:55
  111.6 5.7 %select_add_fusion.w_ref = bf16[3,2304,256]{2,1,0:T(8,128)(2,1)} fusion(bf16[3,2304,256]{2,1,0:T(8,128)(2,1)} %broadcast_in_dim.113, bf16[3,2304,256]{2,1,0:T(8,128)(2,1)} %broadcast_in_dim.107, bf16[3,2304,256]{2,1,0:T(8,128)(2,1)S(1)} %broadcast_in_dim.100, pred[2304,256]{1,0:T(8,128)(4,1)} %broadcast_in_dim.109, pred[2304,256]{1,0:T(8,128)(4,1)} %broadcast_in_dim.103, ...), kind=kLoop, calls=%fused_computation.6 | loop fusion | flops 8847360 | bytes 15925248 | tf_op jit(solution)/shard_map/add | solution.py:55
  118.8 3.7 %copy.44 = bf16[40,1,16,16,16]{0,1,4,3,2:T(2,128)(2,1)} copy(bf16[40,1,16,16,16]{0,4,3,2,1:T(8,128)(2,1)S(1)} %bitcast.59) | data formatting | bytes 655360 | tf_op jit(solution)/shard_map/concatenate | solution.py:85
  124.2 11.8 %maximum_convert_fusion = bf16[40,8,8,8,32]{0,4,3,2,1:T(8,128)(2,1)} fusion(f32[32]{0:T(128)S(1)} %slice_bitcast_fusion.3, bf16[40,2,16,16,16]{0,1,4,3,2:T(2,128)(2,1)S(1)} %bitcast.60, bf16[40,1,16,16,16]{0,1,4,3,2:T(2,128)(2,1)} %copy.44, bf16[32,3,2,2,2]{0,4,3,2,1:T(2,128)(2,1)S(1)} %bitcast.64), kind=kOutput, calls=%fused_computation | convolution fusion | flops 35389440 | bytes 2295424 | tf_op jit(solution)/shard_map/conv_general_dilated | solution.py:88
  136.0 10.7 %copy.46 = bf16[40,8,8,8,32]{4,3,2,1,0:T(8,128)(2,1)} copy(bf16[40,8,8,8,32]{0,4,3,2,1:T(8,128)(2,1)} %maximum_convert_fusion) | data formatting | bytes 2621440 | tf_op jit(solution)/shard_map/convert_element_type | solution.py:96
  146.7 7.3 %reshape.139.h_ref = bf16[2560,256]{1,0:T(8,128)(2,1)} reshape(bf16[40,8,8,8,32]{4,3,2,1,0:T(8,128)(2,1)} %copy.46) | data formatting | bytes 2621440 | tf_op jit(solution)/shard_map/reshape | solution.py:97
  154.7 19.8 %shard_map.104 = bf16[2560,256]{1,0:T(8,128)(2,1)} custom-call(bf16[2560,256]{1,0:T(8,128)(2,1)} %reshape.139.h_ref, bf16[3,2304,256]{2,1,0:T(8,128)(2,1)} %select_add_fusion.w_ref, f32[3,1,256]{2,1,0:T(1,128)} %tile.9.b_ref), custom_call_target="tpu_custom_call" | custom-call | tf_op jit(solution)/shard_map/pallas_call | solution.py:59
  176.1 2.9 %reshape.144 = f32[40,64,8,32]{1,0,3,2:T(8,128)} reshape(f32[2560,256]{0,1:T(8,128)S(1)} %copy.50) | data formatting | bytes 5242880 | tf_op jit(solution)/shard_map/convert_element_type | solution.py:104
  178.9 2.5 %copy.51 = bf16[1,1,40,2,4096]{2,4,3,1,0:T(8,128)(2,1)} copy(bf16[1,1,40,2,4096]{4,3,2,1,0:T(2,128)(2,1)S(1)} %copy-done.1) | data formatting | bytes 1310720 | tf_op args[1]
  184.8 3.1 %multiply_reduce_fusion = f32[40,32]{0,1:T(8,128)S(1)} fusion(f32[40,64,8,32]{1,0,3,2:T(8,128)} %reshape.144, f32[40,64,8]{1,0,2:T(8,128)S(1)} %copy.52), kind=kLoop, calls=%fused_computation.1 | loop fusion | flops 1309440 | bytes 2708480 | tf_op jit(solution)/shard_map/reduce_sum | solution.py:104
  191.1 26.7 %all_gather.3 = bf16[640,129]{1,0:T(8,128)(2,1)S(1)} all-gather(bf16[40,129]{1,0:T(8,128)(2,1)S(1)} %pad_maximum_fusion), channel_id=1, replica_groups=mesh['bulk'=32,'seg'=16] {'seg'}, dimensions={0}, use_global_device_ids=true | all-gather | bytes 175440 | tf_op jit(solution)/shard_map/all_gather | solution.py:139
  (38 shorter events, 16.2 us)
Async XLA Ops:
  0.6 189.4 %copy-start = (bf16[32,128]{1,0:T(8,128)(2,1)S(1)}, bf16[32,128]{1,0:T(8,128)(2,1)}, u32[]{:S(2)}) copy-start(bf16[32,128]{1,0:T(8,128)(2,1)} %param.17) | copy-start | bytes 24580
  117.3 5.2 %copy-start.1 = (bf16[1,1,40,2,4096]{4,3,2,1,0:T(2,128)(2,1)S(1)}, bf16[1,1,40,2,4096]{4,3,2,1,0:T(2,128)(2,1)}, u32[]{:S(2)}) copy-start(bf16[1,1,40,2,4096]{4,3,2,1,0:T(2,128)(2,1)} %param.10) | copy-start | bytes 1966084
  117.3 6.9 %copy-start.2 = (f32[4,32]{1,0:T(4,128)S(1)}, f32[4,32]{1,0:T(4,128)}, u32[]{:S(2)}) copy-start(f32[4,32]{1,0:T(4,128)} %param.15) | copy-start | bytes 1540
  117.3 6.9 %copy-start.4 = (bf16[32,24]{0,1:T(8,128)(2,1)S(1)}, bf16[32,24]{0,1:T(8,128)(2,1)}, u32[]{:S(2)}) copy-start(bf16[32,24]{0,1:T(8,128)(2,1)} %param.13) | copy-start | bytes 4612
  184.6 3.4 %copy-start.5 = (f32[32]{0:T(128)S(1)}, f32[32]{0:T(128)}, u32[]{:S(2)}) copy-start(f32[32]{0:T(128)} %param.16) | copy-start | bytes 388
  184.6 5.7 %copy-start.3 = (s32[1,1,40]{2,1,0:T(1,128)S(1)}, s32[1,1,40]{2,1,0:T(1,128)}, u32[]{:S(2)}) copy-start(s32[1,1,40]{2,1,0:T(1,128)} %param.12) | copy-start | bytes 484
where the time goes:
time: 221 us; the launch traced here: 219 us
  local copies, waits for them, and re-layouts  144 us (65%)
  blocking collectives  26.7 us (12%)
  Pallas kernels  19.8 us (9%)
  matrix products  14.1 us (6%)
  other arithmetic  13.6 us (6%)
    broadcast_in_dim x16, local copies, waits for them, and re-layouts, conv_layers(): jnp.where(hit, taps[:, :, :, shift_c][:, :, :, None, :, None, :], 0)  110 us
    all_gather x1, blocking collectives, per_device(): gathered = lax.all_gather(packed, 'seg', tiled=True)  26.7 us
    pallas_call x1, Pallas kernels, conv_layers(): pl.pallas_call(conv_kernel, grid=(total_rows // block_rows,), in_specs=[p...  19.8 us
    conv_general_dilated x1, matrix products, run_network(): lax.conv_general_dilated(volume_in, patch_kernel, (2, 2, 2), 'VALID', dim...  11.8 us
    convert_element_type x1, local copies, waits for them, and re-layouts, run_network(): volume = jax.nn.relu(first_out + conv_bias[0]).astype(jnp.bfloat16)  10.7 us
    reshape x1, local copies, waits for them, and re-layouts, run_network(): volume = volume.reshape(rows_here * side_half * side_half, lanes)  7.34 us
    unnamed x15, local copies, waits for them, and re-layouts  5.69 us
    add x1, other arithmetic, conv_layers(): band + jnp.where(hit, taps[:, :, :, shift_c][:, :, :, None, :, None, :], 0)  5.67 us

commit v1 on v0

--- a/solution.py
+++ b/solution.py
@@ -12,10 +12,41 @@
 PAD_ROWS = 16
 
 
-def conv_kernel(h_ref, w_ref, b_ref, o_ref, pad_ref, col_ref):
+def conv_kernel(h_ref, w_ref, b_ref, o_ref, pad_ref, col_ref, band_ref):
     rows, lanes = h_ref.shape
     side = CS // 2
+    channels = w_ref.shape[2]
     edge = PAD_ROWS
+
+    @pl.when(pl.program_id(0) == 0)
+    def _():
+        out_lane = lax.broadcasted_iota(jnp.int32, (channels, lanes), 1)
+        in_row = lax.broadcasted_iota(jnp.int32, (channels, lanes), 0)
+        spread = (out_lane % channels == in_row).astype(jnp.bfloat16)
+        z_lane = out_lane // channels
+        for layer_index in range(LAYERS):
+            for tap in range(9):
+                tiled = [
+                    jnp.dot(
+                        w_ref[layer_index, tap * 3 + shift_c],
+                        spread,
+                        preferred_element_type=jnp.float32,
+                    )
+                    for shift_c in range(3)
+                ]
+                for z_in in range(side):
+                    block = jnp.where(
+                        z_lane == z_in + 1,
+                        tiled[0],
+                        jnp.where(
+                            z_lane == z_in,
+                            tiled[1],
+                            jnp.where(z_lane == z_in - 1, tiled[2], 0.0),
+                        ),
+                    )
+                    start = tap * lanes + z_in * channels
+                    band_ref[layer_index, start:start + channels, :] = block.astype(jnp.bfloat16)
+
     pad_ref[0:edge, :] = jnp.zeros((edge, lanes), jnp.float32)
     pad_ref[edge + rows:, :] = jnp.zeros((edge, lanes), jnp.float32)
     pad_ref[edge:edge + rows, :] = h_ref[...].astype(jnp.float32)
@@ -34,7 +65,7 @@
                 col_ref[:, tap * lanes:(tap + 1) * lanes] = jnp.where(
                     inside, window, 0.0
                 ).astype(jnp.bfloat16)
-        summed = jnp.dot(col_ref[...], w_ref[layer_index], preferred_element_type=jnp.float32)
+        summed = jnp.dot(col_ref[...], band_ref[layer_index], preferred_element_type=jnp.float32)
         hidden = jnp.maximum(summed + b_ref[layer_index], 0.0).astype(jnp.bfloat16)
         if layer_index + 1 < LAYERS:
             pad_ref[edge:edge + rows, :] = hidden.astype(jnp.float32)
@@ -46,14 +77,7 @@
     total_rows, lanes = volume.shape
     side = CS // 2
     channels = conv_weight.shape[2]
-    taps = conv_weight.reshape(LAYERS, 3, 3, 3, channels, channels).transpose(0, 1, 2, 3, 5, 4)
-    z_in = jnp.arange(side)[:, None, None, None]
-    z_out = jnp.arange(side)[None, None, :, None]
-    band = jnp.zeros((LAYERS, 3, 3, side, channels, side, channels), jnp.bfloat16)
-    for shift_c in range(3):
-        hit = z_in - z_out + 1 == shift_c
-        band = band + jnp.where(hit, taps[:, :, :, shift_c][:, :, :, None, :, None, :], 0)
-    band = band.reshape(LAYERS, 9 * lanes, lanes)
+    taps = conv_weight.transpose(0, 1, 3, 2)
     bias = jnp.tile(conv_bias[1:], (1, side)).reshape(LAYERS, 1, lanes)
     block_rows = BLOCK_PAIRS * side * side
     return pl.pallas_call(
@@ -61,7 +85,7 @@
         grid=(total_rows // block_rows,),
         in_specs=[
             pl.BlockSpec((block_rows, lanes), lambda i: (i, 0)),
-            pl.BlockSpec((LAYERS, 9 * lanes, lanes), lambda i: (0, 0, 0)),
+            pl.BlockSpec((LAYERS, 27, channels, channels), lambda i: (0, 0, 0, 0)),
             pl.BlockSpec((LAYERS, 1, lanes), lambda i: (0, 0, 0)),
         ],
         out_specs=pl.BlockSpec((block_rows, lanes), lambda i: (i, 0)),
@@ -69,8 +93,10 @@
         scratch_shapes=[
             pltpu.VMEM((block_rows + 2 * PAD_ROWS, lanes), jnp.float32),
             pltpu.VMEM((block_rows, 9 * lanes), jnp.bfloat16),
+            pltpu.VMEM((LAYERS, 9 * lanes, lanes), jnp.bfloat16),
         ],
-    )(volume, band, bias)
+        compiler_params=pltpu.CompilerParams(dimension_semantics=("arbitrary",)),
+    )(volume, taps, bias)
 
 
 def run_network(

time: 221 us -> 107 us (0.48)
  local copies, waits for them, and re-layouts: 144 us -> 37.8 us
  other arithmetic: 13.6 us -> 7.83 us
    broadcast_in_dim x16 -> x0, local copies, waits for them, and re-layouts: 110 us -> none  [conv_layers(): jnp.where(hit, taps[:, :, :, shift_c][:, :, :, None, :, None, :], 0)]
    add x1 -> x0, other arithmetic: 5.67 us -> none  [conv_layers(): band + jnp.where(hit, taps[:, :, :, shift_c][:, :, :, None, :, None, :], 0)]
    unnamed x15 -> x18, local copies, waits for them, and re-layouts: 5.69 us -> 9.93 us
where the time goes in v1:
time: 107 us; the launch traced here: 106 us
  local copies, waits for them, and re-layouts  37.8 us (35%)
  blocking collectives  26.7 us (25%)
  Pallas kernels  19.8 us (19%)
  matrix products  12.7 us (12%)
  other arithmetic  7.83 us (7%)
    all_gather x1, blocking collectives, per_device(): gathered = lax.all_gather(packed, 'seg', tiled=True)  26.7 us
    pallas_call x1, Pallas kernels, conv_layers(): pl.pallas_call(conv_kernel, grid=(total_rows // block_rows,), in_specs=[p...  19.8 us
    convert_element_type x1, local copies, waits for them, and re-layouts, run_network(): volume = jax.nn.relu(first_out + conv_bias[0]).astype(jnp.bfloat16)  10.7 us
    conv_general_dilated x1, matrix products, run_network(): lax.conv_general_dilated(volume_in, patch_kernel, (2, 2, 2), 'VALID', dim...  10.4 us
    unnamed x18, local copies, waits for them, and re-layouts  9.93 us
    reshape x1, local copies, waits for them, and re-layouts, run_network(): volume = volume.reshape(rows_here * side_half * side_half, lanes)  7.41 us
    convert_element_type x2, local copies, waits for them, and re-layouts, run_network(): hidden.astype(jnp.float32) * boundary[..., None]  4.66 us
    reduce_sum x1, other arithmetic, run_network(): jnp.sum(hidden.astype(jnp.float32) * boundary[..., None], axis=(1, 2))  3.14 us

profile of v1, /device:TPU:2, one launch (start us, length us, event | category | flops | bytes accessed | tf_op | source)
XLA Modules:
  0.0 105.6 jit_solution(1540326563547946098)
XLA Ops:
  0.7 1.3 %dynamic_slice.3 = s32[1,1]{0,1:T(1,128)} dynamic-slice(s32[32,16]{0,1:T(8,128)} %param.11, s32[]{:T(128)S(6)} %select_n.25, s32[]{:T(128)S(6)} %select_n.26), dynamic_slice_sizes={1,1} | dynamic-slice | bytes 12 | tf_op jit(solution)/shard_map/dynamic_slice | solution.py:155
  2.0 0.7 slice_bitcast_fusion
  2.7 4.8 %copy.37 = bf16[1,1,40,2,4096]{2,3,4,1,0:T(2,128)(2,1)S(1)} copy(bf16[1,1,40,2,4096]{4,3,2,1,0:T(2,128)(2,1)} %param.10) | data formatting | bytes 1310720 | tf_op args[1]
  7.5 1.4 %copy.36 = bf16[1,1,40,4096]{2,3,1,0:T(8,128)(2,1)S(1)} copy(bf16[1,1,40,4096]{3,2,1,0:T(8,128)(2,1)} %param.9) | data formatting | bytes 655360 | tf_op args[0]
  9.0 2.2 %copy.38 = bf16[40,1,16,16,16]{0,1,4,3,2:T(2,128)(2,1)S(1)} copy(bf16[40,1,16,16,16]{0,4,3,2,1:T(8,128)(2,1)S(1)} %bitcast.39) | data formatting | bytes 655360 | tf_op jit(solution)/shard_map/concatenate | solution.py:111
  11.2 10.4 %maximum_convert_fusion = bf16[40,8,8,8,32]{0,4,3,2,1:T(8,128)(2,1)} fusion(f32[32]{0:T(128)S(1)} %slice_bitcast_fusion, bf16[40,2,16,16,16]{0,1,4,3,2:T(2,128)(2,1)S(1)} %bitcast.41, bf16[40,1,16,16,16]{0,1,4,3,2:T(2,128)(2,1)S(1)} %copy.38, bf16[32,3,2,2,2]{0,4,3,2,1:T(2,128)(2,1)S(1)} %bitcast.44), kind=kOutput, calls=%fused_computation | convolution fusion | flops 35389440 | bytes 2295424 | tf_op jit(solution)/shard_map/conv_general_dilated | solution.py:114
  21.5 10.7 %copy.40 = bf16[40,8,8,8,32]{4,3,2,1,0:T(8,128)(2,1)} copy(bf16[40,8,8,8,32]{0,4,3,2,1:T(8,128)(2,1)} %maximum_convert_fusion) | data formatting | bytes 2621440 | tf_op jit(solution)/shard_map/convert_element_type | solution.py:122
  32.2 7.4 %reshape.89.h_ref = bf16[2560,256]{1,0:T(8,128)(2,1)} reshape(bf16[40,8,8,8,32]{4,3,2,1,0:T(8,128)(2,1)} %copy.40) | data formatting | bytes 2621440 | tf_op jit(solution)/shard_map/reshape | solution.py:123
  39.7 1.1 %copy.41 = bf16[3,27,32,32]{2,3,1,0:T(8,128)(2,1)} copy(bf16[3,27,32,32]{3,2,1,0:T(8,128)(2,1)S(1)} %copy-done.2) | data formatting | bytes 331776 | tf_op args[5]
  40.8 0.7 tile.9.b_ref
  41.5 19.8 %shard_map.104 = bf16[2560,256]{1,0:T(8,128)(2,1)} custom-call(bf16[2560,256]{1,0:T(8,128)(2,1)} %reshape.89.h_ref, bf16[3,27,32,32]{3,2,1,0:T(8,128)(2,1)} %bitcast.40, f32[3,1,256]{2,1,0:T(1,128)} %tile.9.b_ref), custom_call_target="tpu_custom_call" | custom-call | tf_op jit(solution)/shard_map/pallas_call | solution.py:83
  61.3 1.6 %copy.42 = f32[2560,256]{0,1:T(8,128)S(1)} copy(bf16[2560,256]{1,0:T(8,128)(2,1)} %shard_map.104) | data formatting | bytes 3932160 | tf_op jit(solution)/shard_map/convert_element_type | solution.py:130
  62.9 3.1 %reshape.93 = f32[40,64,8,32]{1,0,3,2:T(8,128)} reshape(f32[2560,256]{0,1:T(8,128)S(1)} %copy.42) | data formatting | bytes 5242880 | tf_op jit(solution)/shard_map/convert_element_type | solution.py:130
  66.0 2.5 %copy.43 = bf16[1,1,40,2,4096]{2,4,3,1,0:T(8,128)(2,1)} copy(bf16[1,1,40,2,4096]{4,3,2,1,0:T(2,128)(2,1)S(1)} %copy-done.1) | data formatting | bytes 1310720 | tf_op args[1]
  68.5 1.7 %convert_multiply_fusion = f32[40,1,4096]{0,2,1:T(8,128)S(1)} fusion(bf16[40,2,4096]{0,2,1:T(8,128)(2,1)} %bitcast.38), kind=kLoop, calls=%fused_computation.6 | loop fusion | flops 491520 | bytes 1310720 | tf_op jit(solution)/shard_map/mul | solution.py:126
  70.2 1.4 %reduce_sum.27 = f32[40,8,8,8]{0,3,2,1:T(8,128)S(1)} reduce(f32[40,8,2,8,2,8,2]{0,6,5,4,3,2,1:T(2,128)S(1)} %bitcast.37, f32[]{:T(128)} %constant.26.clone.1), dimensions={2,4,6}, to_apply=%region_0.1 | reduce | flops 143360 | bytes 737284 | tf_op jit(solution)/shard_map/reduce_sum | solution.py:128
  71.9 3.1 %multiply_reduce_fusion = f32[40,32]{0,1:T(8,128)S(1)} fusion(f32[40,64,8,32]{1,0,3,2:T(8,128)} %reshape.93, f32[40,64,8]{1,0,2:T(8,128)S(1)} %copy.44), kind=kLoop, calls=%fused_computation.1 | loop fusion | flops 1309440 | bytes 2708480 | tf_op jit(solution)/shard_map/reduce_sum | solution.py:130
  75.0 1.3 %fusion.23 = (f32[40]{0:T(128)S(1)}, bf16[1,1,40]{2,1,0:T(2,128)(2,1)}) fusion(s32[]{:T(128)} %bitcast, f32[32]{0:T(128)S(1)} %copy-done.6, f32[40,32]{0,1:T(8,128)S(1)} %multiply_reduce_fusion, f32[40]{0:T(128)S(1)} %get-tuple-element.2), kind=kOutput, calls=%fused_computation.36 | convolution fusion | flops 16920 | bytes 5652 | tf_op jit(solution)/shard_map/dot_general | solution.py:132
  76.4 0.6 select_convert_fusion
  77.0 0.6 iota_compare_fusion.1
  77.7 0.2 fusion.8
  77.9 26.7 %all_gather.3 = bf16[640,129]{1,0:T(8,128)(2,1)S(1)} all-gather(bf16[40,129]{1,0:T(8,128)(2,1)S(1)} %pad_maximum_fusion), channel_id=1, replica_groups=mesh['bulk'=32,'seg'=16] {'seg'}, dimensions={0}, use_global_device_ids=true | all-gather | bytes 175440 | tf_op jit(solution)/shard_map/all_gather | solution.py:165
  104.6 0.2 convert_reduce_fusion
  104.8 0.8 fusion.14
  (21 shorter events, 0.4 us)
Async XLA Ops:
  0.6 77.0 %copy-start = (bf16[32,128]{1,0:T(8,128)(2,1)S(1)}, bf16[32,128]{1,0:T(8,128)(2,1)}, u32[]{:S(2)}) copy-start(bf16[32,128]{1,0:T(8,128)(2,1)} %param.17) | copy-start | bytes 24580
  0.6 10.5 %copy-start.5 = (bf16[32,24]{0,1:T(8,128)(2,1)S(1)}, bf16[32,24]{0,1:T(8,128)(2,1)}, u32[]{:S(2)}) copy-start(bf16[32,24]{0,1:T(8,128)(2,1)} %param.13) | copy-start | bytes 4612
  32.2 7.4 %copy-start.2 = (bf16[3,27,32,32]{3,2,1,0:T(8,128)(2,1)S(1)}, bf16[3,27,32,32]{3,2,1,0:T(8,128)(2,1)}, u32[]{:S(2)}) copy-start(bf16[3,27,32,32]{3,2,1,0:T(8,128)(2,1)} %param.14) | copy-start | bytes 497668
  32.2 8.5 %copy-start.3 = (f32[4,32]{1,0:T(4,128)S(1)}, f32[4,32]{1,0:T(4,128)}, u32[]{:S(2)}) copy-start(f32[4,32]{1,0:T(4,128)} %param.15) | copy-start | bytes 1540
  62.9 3.1 %copy-start.1 = (bf16[1,1,40,2,4096]{4,3,2,1,0:T(2,128)(2,1)S(1)}, bf16[1,1,40,2,4096]{4,3,2,1,0:T(2,128)(2,1)}, u32[]{:S(2)}) copy-start(bf16[1,1,40,2,4096]{4,3,2,1,0:T(2,128)(2,1)} %param.10) | copy-start | bytes 1966084
  70.2 4.8 %copy-start.6 = (f32[32]{0:T(128)S(1)}, f32[32]{0:T(128)}, u32[]{:S(2)}) copy-start(f32[32]{0:T(128)} %param.16) | copy-start | bytes 388
  70.2 6.1 %copy-start.4 = (s32[1,1,40]{2,1,0:T(1,128)S(1)}, s32[1,1,40]{2,1,0:T(1,128)}, u32[]{:S(2)}) copy-start(s32[1,1,40]{2,1,0:T(1,128)} %param.12) | copy-start | bytes 484

commit v2 on v1

--- a/solution.py
+++ b/solution.py
@@ -12,8 +12,8 @@
 PAD_ROWS = 16
 
 
-def conv_kernel(h_ref, w_ref, b_ref, o_ref, pad_ref, col_ref, band_ref):
-    rows, lanes = h_ref.shape
+def conv_kernel(x_ref, q_ref, first_bias_ref, w_ref, b_ref, o_ref, pad_ref, col_ref, band_ref):
+    rows, lanes = o_ref.shape
     side = CS // 2
     channels = w_ref.shape[2]
     edge = PAD_ROWS
@@ -49,7 +49,9 @@
 
     pad_ref[0:edge, :] = jnp.zeros((edge, lanes), jnp.float32)
     pad_ref[edge + rows:, :] = jnp.zeros((edge, lanes), jnp.float32)
-    pad_ref[edge:edge + rows, :] = h_ref[...].astype(jnp.float32)
+    first = jnp.dot(x_ref[...], q_ref[...], preferred_element_type=jnp.float32)
+    first = jnp.maximum(first + first_bias_ref[...], 0.0).astype(jnp.bfloat16)
+    pad_ref[edge:edge + rows, :] = first.astype(jnp.float32)
     row_id = lax.broadcasted_iota(jnp.int32, (rows, lanes), 0)
     y_pos = row_id % side
     x_pos = (row_id // side) % side
@@ -73,10 +75,18 @@
             o_ref[...] = hidden
 
 
-def conv_layers(volume, conv_weight, conv_bias):
-    total_rows, lanes = volume.shape
+def conv_layers(features, patch_weight, conv_weight, conv_bias):
+    total_rows, feature_count = features.shape
     side = CS // 2
     channels = conv_weight.shape[2]
+    lanes = side * channels
+    per_cell = patch_weight.reshape(channels, 3, 2, 2, 2).transpose(1, 2, 3, 4, 0)
+    z_in = jnp.arange(side)[:, None, None, None]
+    z_out = jnp.arange(side)[None, None, :, None]
+    patch_matrix = jnp.where(
+        z_in == z_out, per_cell[:, :, :, None, :, None, :], 0
+    ).reshape(feature_count, lanes)
+    first_bias = jnp.tile(conv_bias[0], side).reshape(1, lanes)
     taps = conv_weight.transpose(0, 1, 3, 2)
     bias = jnp.tile(conv_bias[1:], (1, side)).reshape(LAYERS, 1, lanes)
     block_rows = BLOCK_PAIRS * side * side
@@ -84,7 +94,9 @@
         conv_kernel,
         grid=(total_rows // block_rows,),
         in_specs=[
-            pl.BlockSpec((block_rows, lanes), lambda i: (i, 0)),
+            pl.BlockSpec((block_rows, feature_count), lambda i: (i, 0)),
+            pl.BlockSpec((feature_count, lanes), lambda i: (0, 0)),
+            pl.BlockSpec((1, lanes), lambda i: (0, 0)),
             pl.BlockSpec((LAYERS, 27, channels, channels), lambda i: (0, 0, 0, 0)),
             pl.BlockSpec((LAYERS, 1, lanes), lambda i: (0, 0, 0)),
         ],
@@ -96,7 +108,7 @@
             pltpu.VMEM((LAYERS, 9 * lanes, lanes), jnp.bfloat16),
         ],
         compiler_params=pltpu.CompilerParams(dimension_semantics=("arbitrary",)),
-    )(volume, taps, bias)
+    )(features, patch_matrix, first_bias, taps, bias)
 
 
 def run_network(
@@ -109,19 +121,9 @@
     lanes = side_half * channels
     highest = lax.Precision.HIGHEST
     stacked = jnp.concatenate([em_rows[:, None, :], mask_rows], axis=1)
-    volume_in = stacked.reshape(rows_here, 3, CS, CS, CS)
-    patch_kernel = patch_weight.reshape(channels, 3, 2, 2, 2)
-    first_out = lax.conv_general_dilated(
-        volume_in,
-        patch_kernel,
-        (2, 2, 2),
-        "VALID",
-        dimension_numbers=("NCDHW", "OIDHW", "NDHWC"),
-        preferred_element_type=jnp.float32,
-    )
-    volume = jax.nn.relu(first_out + conv_bias[0]).astype(jnp.bfloat16)
-    volume = volume.reshape(rows_here * side_half * side_half, lanes)
-    hidden = conv_layers(volume, conv_weight, conv_bias)
+    cells = stacked.reshape(rows_here, 3, side_half, 2, side_half, 2 * CS)
+    features = cells.transpose(0, 2, 4, 1, 3, 5).reshape(rows_here * side_half * side_half, 12 * CS)
+    hidden = conv_layers(features, patch_weight, conv_weight, conv_bias)
     hidden = hidden.reshape(rows_here, side_half * side_half, side_half, channels)
     intersection = mask_rows[:, 0].astype(jnp.float32) * mask_rows[:, 1].astype(jnp.float32)
     intersection = intersection.reshape(rows_here, side_half, 2, side_half, 2, side_half, 2)

time: 107 us -> 92.4 us (0.86)
  matrix products: 12.7 us -> 2.27 us
  local copies, waits for them, and re-layouts: 37.8 us -> 31.6 us
  other arithmetic: 7.83 us -> 9.91 us
    convert_element_type x1 -> x0, local copies, waits for them, and re-layouts: 10.7 us -> none  [run_network(): volume = jax.nn.relu(first_out + conv_bias[0]).astype(jnp.bfloat16)]
    conv_general_dilated x1 -> x0, matrix products: 10.4 us -> none  [run_network(): lax.conv_general_dilated(volume_in, patch_kernel, (2, 2, 2), 'VALID', dim...]
    transpose x0 -> x1, local copies, waits for them, and re-layouts: none -> 5.99 us  [run_network(): cells.transpose(0, 2, 4, 1, 3, 5)]
    unnamed x18 -> x19, local copies, waits for them, and re-layouts: 9.93 us -> 5.47 us
    concatenate x1 -> x2, local copies, waits for them, and re-layouts: 2.17 us -> 4.94 us  [run_network(): stacked = jnp.concatenate([em_rows[:, None, :], mask_rows], axis=1)]
    transpose x0 -> x1, other arithmetic: none -> 2.08 us  [run_network(): cells.transpose(0, 2, 4, 1, 3, 5)]
    reshape x1, local copies, waits for them, and re-layouts: 7.41 us -> 6.22 us  [run_network(): cells.transpose(0, 2, 4, 1, 3, 5)]
where the time goes in v2:
time: 92.4 us; the launch traced here: 91.9 us
  local copies, waits for them, and re-layouts  31.6 us (34%)
  blocking collectives  26.7 us (29%)
  Pallas kernels  20.7 us (22%)
  other arithmetic  9.91 us (11%)
  matrix products  2.27 us (2%)
    all_gather x1, blocking collectives, per_device(): gathered = lax.all_gather(packed, 'seg', tiled=True)  26.7 us
    pallas_call x1, Pallas kernels, conv_layers(): pl.pallas_call(conv_kernel, grid=(total_rows // block_rows,), in_specs=[p...  20.7 us
    reshape x1, local copies, waits for them, and re-layouts, run_network(): cells.transpose(0, 2, 4, 1, 3, 5)  6.22 us
    transpose x1, local copies, waits for them, and re-layouts, run_network(): cells.transpose(0, 2, 4, 1, 3, 5)  5.99 us
    unnamed x19, local copies, waits for them, and re-layouts  5.47 us
    concatenate x2, local copies, waits for them, and re-layouts, run_network(): stacked = jnp.concatenate([em_rows[:, None, :], mask_rows], axis=1)  4.94 us
    convert_element_type x2, local copies, waits for them, and re-layouts, run_network(): hidden.astype(jnp.float32) * boundary[..., None]  4.48 us
    reduce_sum x1, other arithmetic, run_network(): jnp.sum(hidden.astype(jnp.float32) * boundary[..., None], axis=(1, 2))  3.14 us

profile of v2, /device:TPU:2, one launch (start us, length us, event | category | flops | bytes accessed | tf_op | source)
XLA Modules:
  0.0 91.9 jit_solution(16013180068513543717)
XLA Ops:
  0.7 1.3 %dynamic_slice.3 = s32[1,1]{0,1:T(1,128)} dynamic-slice(s32[32,16]{0,1:T(8,128)} %param.11, s32[]{:T(128)S(6)} %select_n.33, s32[]{:T(128)S(6)} %select_n.34), dynamic_slice_sizes={1,1} | dynamic-slice | bytes 12 | tf_op jit(solution)/shard_map/dynamic_slice | solution.py:157
  1.9 3.9 %copy.32 = bf16[1,1,40,2,4096]{2,4,3,1,0:T(8,128)(2,1)} copy(bf16[1,1,40,2,4096]{4,3,2,1,0:T(2,128)(2,1)} %param.10) | data formatting | bytes 1310720 | tf_op args[1]
  5.9 1.7 %convert_multiply_fusion = f32[40,1,4096]{0,2,1:T(8,128)S(1)} fusion(bf16[40,2,4096]{0,2,1:T(8,128)(2,1)} %bitcast.46), kind=kLoop, calls=%fused_computation.2 | loop fusion | flops 491520 | bytes 1310720 | tf_op jit(solution)/shard_map/mul | solution.py:128
  7.6 1.4 %reduce_sum.27 = f32[40,8,8,8]{0,3,2,1:T(8,128)S(1)} reduce(f32[40,8,2,8,2,8,2]{0,6,5,4,3,2,1:T(2,128)S(1)} %bitcast.45, f32[]{:T(128)} %constant.25.clone.1), dimensions={2,4,6}, to_apply=%region_0.1 | reduce | flops 143360 | bytes 737284 | tf_op jit(solution)/shard_map/reduce_sum | solution.py:130
  9.1 0.8 copy.33
  9.9 0.4 copy.28
  10.3 2.1 %concatenate.12 = bf16[40,2,8,2,8,32]{5,4,3,2,0,1:T(8,128)(2,1)S(1)} reshape(bf16[1,1,40,2,4096]{4,2,3,1,0:T(8,128)(2,1)S(1)} %copy.28) | data formatting | bytes 1310720 | tf_op jit(solution)/shard_map/concatenate | solution.py:123
  12.4 2.9 %concatenate.11 = bf16[40,1,8,2,8,32]{5,4,3,2,0,1:T(8,128)(2,1)} reshape(bf16[1,1,40,4096]{3,2,1,0:T(8,128)(2,1)} %param.9) | data formatting | bytes 655360 | tf_op jit(solution)/shard_map/concatenate | solution.py:123
  15.3 2.1 %maximum_bitcast_fusion = bf16[40,8,8,3,2,32]{5,2,4,1,0,3:T(8,128)(2,1)S(1)} fusion(bf16[40,2,8,2,8,32]{5,4,3,2,0,1:T(8,128)(2,1)S(1)} %concatenate.12, bf16[40,1,8,2,8,32]{5,4,3,2,0,1:T(8,128)(2,1)} %concatenate.11), kind=kLoop, calls=%fused_computation.1 | loop fusion | flops 491520 | bytes 1966080 | tf_op jit(solution)/shard_map/transpose | solution.py:125
  17.3 6.0 %copy.29 = bf16[40,8,8,3,2,32]{5,4,3,2,1,0:T(2,128)(2,1)} copy(bf16[40,8,8,3,2,32]{5,2,4,1,0,3:T(8,128)(2,1)S(1)} %maximum_bitcast_fusion) | data formatting | bytes 1966080 | tf_op jit(solution)/shard_map/transpose | solution.py:125
  23.3 6.2 %reshape.106.x_ref = bf16[2560,192]{1,0:T(8,128)(2,1)} reshape(bf16[40,8,8,3,2,32]{5,4,3,2,1,0:T(2,128)(2,1)} %copy.29) | data formatting | bytes 1966080 | tf_op jit(solution)/shard_map/reshape | solution.py:125
  29.6 1.1 %copy.30 = bf16[3,27,32,32]{2,3,1,0:T(8,128)(2,1)} copy(bf16[3,27,32,32]{3,2,1,0:T(8,128)(2,1)S(1)} %copy-done.2) | data formatting | bytes 331776 | tf_op args[5]
  30.8 0.9 %select_n.36.q_ref = bf16[192,256]{1,0:T(8,128)(2,1)} reshape(bf16[3,2,2,8,2,8,32]{6,5,4,3,2,1,0:T(8,128)(2,1)S(1)} %broadcast_select_fusion) | data formatting | bytes 196608 | tf_op jit(solution)/shard_map/jit(_where)/select_n | solution.py:86
  31.8 0.7 tile.18.b_ref
  32.4 0.7 reshape_tile.4.first_bias_ref
  33.1 20.7 %shard_map.104 = bf16[2560,256]{1,0:T(8,128)(2,1)} custom-call(bf16[2560,192]{1,0:T(8,128)(2,1)} %reshape.106.x_ref, bf16[192,256]{1,0:T(8,128)(2,1)} %select_n.36.q_ref, f32[1,256]{1,0:T(1,128)} %reshape_tile.4.first_bias_ref, bf16[3,27,32,32]{3,2,1,0:T(8,128)(2,1)} %bitcast.47, f32[3,1,256]{2,1,0:T(1,128)} %tile.18.b_ref), custom_call_target="tpu_custom_call" | custom-call | tf_op jit(solution)/shard_map/pallas_call | solution.py:93
  53.8 1.6 %copy.31 = f32[2560,256]{0,1:T(8,128)S(1)} copy(bf16[2560,256]{1,0:T(8,128)(2,1)} %shard_map.104) | data formatting | bytes 3932160 | tf_op jit(solution)/shard_map/convert_element_type | solution.py:132
  55.4 2.9 %reshape.111 = f32[40,64,8,32]{1,0,3,2:T(8,128)} reshape(f32[2560,256]{0,1:T(8,128)S(1)} %copy.31) | data formatting | bytes 5242880 | tf_op jit(solution)/shard_map/convert_element_type | solution.py:132
  58.3 3.1 %multiply_reduce_fusion = f32[40,32]{0,1:T(8,128)S(1)} fusion(f32[40,64,8,32]{1,0,3,2:T(8,128)} %reshape.111, f32[40,64,8]{1,0,2:T(8,128)S(1)} %copy-done.3), kind=kLoop, calls=%fused_computation | loop fusion | flops 1309440 | bytes 2708480 | tf_op jit(solution)/shard_map/reduce_sum | solution.py:132
  61.5 1.2 %fusion.15 = (f32[40]{0:T(128)S(1)}, bf16[1,1,40]{2,1,0:T(2,128)(2,1)}) fusion(s32[]{:T(128)} %bitcast, f32[32]{0:T(128)S(1)} %copy-done.7, f32[40,32]{0,1:T(8,128)S(1)} %multiply_reduce_fusion, f32[40]{0:T(128)S(1)} %get-tuple-element.2), kind=kOutput, calls=%fused_computation.32 | convolution fusion | flops 16920 | bytes 5652 | tf_op jit(solution)/shard_map/dot_general | solution.py:134
  62.7 0.6 iota_compare_fusion.2
  63.6 0.6 select_convert_fusion
  64.2 26.7 %all_gather.3 = bf16[640,129]{1,0:T(8,128)(2,1)S(1)} all-gather(bf16[40,129]{1,0:T(8,128)(2,1)S(1)} %pad_maximum_fusion), channel_id=1, replica_groups=mesh['bulk'=32,'seg'=16] {'seg'}, dimensions={0}, use_global_device_ids=true | all-gather | bytes 175440 | tf_op jit(solution)/shard_map/all_gather | solution.py:167
  91.1 0.8 fusion.8
  (28 shorter events, 0.8 us)
Async XLA Ops:
  0.6 62.7 %copy-start = (bf16[32,128]{1,0:T(8,128)(2,1)S(1)}, bf16[32,128]{1,0:T(8,128)(2,1)}, u32[]{:S(2)}) copy-start(bf16[32,128]{1,0:T(8,128)(2,1)} %param.17) | copy-start | bytes 24580
  7.6 2.3 %copy-start.1 = (bf16[1,1,40,2,4096]{4,3,2,1,0:T(2,128)(2,1)S(1)}, bf16[1,1,40,2,4096]{4,3,2,1,0:T(2,128)(2,1)}, u32[]{:S(2)}) copy-start(bf16[1,1,40,2,4096]{4,3,2,1,0:T(2,128)(2,1)} %param.10) | copy-start | bytes 1966084
  23.3 6.2 %copy-start.2 = (bf16[3,27,32,32]{3,2,1,0:T(8,128)(2,1)S(1)}, bf16[3,27,32,32]{3,2,1,0:T(8,128)(2,1)}, u32[]{:S(2)}) copy-start(bf16[3,27,32,32]{3,2,1,0:T(8,128)(2,1)} %param.14) | copy-start | bytes 497668
  23.3 7.4 %copy-start.4 = (bf16[32,24]{0,1:T(8,128)(2,1)S(1)}, bf16[32,24]{0,1:T(8,128)(2,1)}, u32[]{:S(2)}) copy-start(bf16[32,24]{0,1:T(8,128)(2,1)} %param.13) | copy-start | bytes 4612
  23.3 8.4 %copy-start.5 = (f32[4,32]{1,0:T(4,128)S(1)}, f32[4,32]{1,0:T(4,128)}, u32[]{:S(2)}) copy-start(f32[4,32]{1,0:T(4,128)} %param.15) | copy-start | bytes 1540
  55.4 2.9 %copy-start.3 = (f32[40,64,8]{1,0,2:T(8,128)S(1)}, f32[40,64,8]{1,0,2:T(8,128)}, u32[]{:S(2)}) copy-start(f32[40,64,8]{1,0,2:T(8,128)} %copy.33) | copy-start | bytes 245764
  58.3 3.1 %copy-start.7 = (f32[32]{0:T(128)S(1)}, f32[32]{0:T(128)}, u32[]{:S(2)}) copy-start(f32[32]{0:T(128)} %param.16) | copy-start | bytes 388
  58.3 5.2 %copy-start.6 = (s32[1,1,40]{2,1,0:T(1,128)S(1)}, s32[1,1,40]{2,1,0:T(1,128)}, u32[]{:S(2)}) copy-start(s32[1,1,40]{2,1,0:T(1,128)} %param.12) | copy-start | bytes 484

commit v3 on v2

--- a/solution.py
+++ b/solution.py
@@ -162,14 +162,14 @@
     )
     scores = jnp.where(live_slot, part_score, 0)
     contribs = jnp.where(live_slot[:, None], part_contrib, 0)
+    n_seg = lax.axis_size("seg")
     seg_local = jnp.where(live_slot, segment_ids.reshape(slots), -1)
-    packed = jnp.concatenate([contribs, seg_local[:, None].astype(jnp.bfloat16)], axis=1)
-    gathered = lax.all_gather(packed, "seg", tiled=True)
-    all_contrib = gathered[:, :-1]
-    all_ids = gathered[:, -1].astype(jnp.int32)
-    wanted = seg_index * SEG_DEV + jnp.arange(SEG_DEV, dtype=jnp.int32)
-    onehot = (all_ids[None, :] == wanted[:, None]).astype(jnp.bfloat16)
-    summed = jnp.dot(onehot, all_contrib, preferred_element_type=jnp.float32)
+    segment_row = jnp.arange(n_seg * SEG_DEV, dtype=jnp.int32)
+    onehot = (segment_row[:, None] == seg_local[None, :]).astype(jnp.bfloat16)
+    partial_value = jnp.dot(onehot, contribs, preferred_element_type=jnp.float32)
+    partial_value = partial_value.reshape(n_seg, SEG_DEV, -1)
+    arrived = lax.all_to_all(partial_value, "seg", 0, 0, tiled=True)
+    summed = jnp.sum(arrived, axis=0)
     return (scores.reshape(1, 1, slots), summed)
 
 

time: 92.4 us -> 79.7 us (0.86)
  blocking collectives: 26.7 us -> 14.6 us
    all_gather x1 -> x0, blocking collectives: 26.7 us -> none  [per_device(): gathered = lax.all_gather(packed, 'seg', tiled=True)]
    all_to_all x0 -> x1, blocking collectives: none -> 14.6 us  [per_device(): arrived = lax.all_to_all(partial_value, 'seg', 0, 0, tiled=True)]
    unnamed x19 -> x17, local copies, waits for them, and re-layouts: 5.47 us -> 5.54 us
where the time goes in v3:
time: 79.7 us; the launch traced here: 79.2 us
  local copies, waits for them, and re-layouts  30.9 us (39%)
  Pallas kernels  20.7 us (26%)
  blocking collectives  14.6 us (18%)
  other arithmetic  10.5 us (13%)
  matrix products  1.68 us (2%)
  between operations  0.8 us (1%)
    pallas_call x1, Pallas kernels, conv_layers(): pl.pallas_call(conv_kernel, grid=(total_rows // block_rows,), in_specs=[p...  20.7 us
    all_to_all x1, blocking collectives, per_device(): arrived = lax.all_to_all(partial_value, 'seg', 0, 0, tiled=True)  14.6 us
    reshape x1, local copies, waits for them, and re-layouts, run_network(): cells.transpose(0, 2, 4, 1, 3, 5)  6.22 us
    transpose x1, local copies, waits for them, and re-layouts, run_network(): cells.transpose(0, 2, 4, 1, 3, 5)  5.99 us
    unnamed x17, local copies, waits for them, and re-layouts  5.54 us
    concatenate x2, local copies, waits for them, and re-layouts, run_network(): stacked = jnp.concatenate([em_rows[:, None, :], mask_rows], axis=1)  4.94 us
    convert_element_type x2, local copies, waits for them, and re-layouts, run_network(): hidden.astype(jnp.float32) * boundary[..., None]  4.48 us
    reduce_sum x1, other arithmetic, run_network(): jnp.sum(hidden.astype(jnp.float32) * boundary[..., None], axis=(1, 2))  3.13 us

profile of v3, /device:TPU:2, one launch (start us, length us, event | category | flops | bytes accessed | tf_op | source)
XLA Modules:
  0.0 79.2 jit_solution(15262096536468034434)
XLA Ops:
  0.7 4.0 %copy.29 = bf16[1,1,40,2,4096]{2,4,3,1,0:T(8,128)(2,1)} copy(bf16[1,1,40,2,4096]{4,3,2,1,0:T(2,128)(2,1)} %param.10) | data formatting | bytes 1310720 | tf_op args[1]
  4.7 0.4 copy.25
  5.1 1.7 %convert_multiply_fusion = f32[40,1,4096]{0,2,1:T(8,128)S(1)} fusion(bf16[40,2,4096]{0,2,1:T(8,128)(2,1)} %bitcast.50), kind=kLoop, calls=%fused_computation.2 | loop fusion | flops 491520 | bytes 1310720 | tf_op jit(solution)/shard_map/mul | solution.py:128
  6.9 1.4 %reduce_sum.36 = f32[40,8,8,8]{0,3,2,1:T(8,128)S(1)} reduce(f32[40,8,2,8,2,8,2]{0,6,5,4,3,2,1:T(2,128)S(1)} %bitcast.49, f32[]{:T(128)} %constant.24.clone.1), dimensions={2,4,6}, to_apply=%region_0.1 | reduce | flops 143360 | bytes 737284 | tf_op jit(solution)/shard_map/reduce_sum | solution.py:130
  8.5 2.1 %concatenate.9 = bf16[40,2,8,2,8,32]{5,4,3,2,0,1:T(8,128)(2,1)S(1)} reshape(bf16[1,1,40,2,4096]{4,2,3,1,0:T(8,128)(2,1)S(1)} %copy.25) | data formatting | bytes 1310720 | tf_op jit(solution)/shard_map/concatenate | solution.py:123
  10.6 2.9 %concatenate.8 = bf16[40,1,8,2,8,32]{5,4,3,2,0,1:T(8,128)(2,1)} reshape(bf16[1,1,40,4096]{3,2,1,0:T(8,128)(2,1)} %param.9) | data formatting | bytes 655360 | tf_op jit(solution)/shard_map/concatenate | solution.py:123
  13.4 2.1 %maximum_bitcast_fusion = bf16[40,8,8,3,2,32]{5,2,4,1,0,3:T(8,128)(2,1)S(1)} fusion(bf16[40,2,8,2,8,32]{5,4,3,2,0,1:T(8,128)(2,1)S(1)} %concatenate.9, bf16[40,1,8,2,8,32]{5,4,3,2,0,1:T(8,128)(2,1)} %concatenate.8), kind=kLoop, calls=%fused_computation.1 | loop fusion | flops 491520 | bytes 1966080 | tf_op jit(solution)/shard_map/transpose | solution.py:125
  15.5 6.0 %copy.26 = bf16[40,8,8,3,2,32]{5,4,3,2,1,0:T(2,128)(2,1)} copy(bf16[40,8,8,3,2,32]{5,2,4,1,0,3:T(8,128)(2,1)S(1)} %maximum_bitcast_fusion) | data formatting | bytes 1966080 | tf_op jit(solution)/shard_map/transpose | solution.py:125
  21.5 6.2 %reshape.88.x_ref = bf16[2560,192]{1,0:T(8,128)(2,1)} reshape(bf16[40,8,8,3,2,32]{5,4,3,2,1,0:T(2,128)(2,1)} %copy.26) | data formatting | bytes 1966080 | tf_op jit(solution)/shard_map/reshape | solution.py:125
  27.7 1.1 %copy.27 = bf16[3,27,32,32]{2,3,1,0:T(8,128)(2,1)} copy(bf16[3,27,32,32]{3,2,1,0:T(8,128)(2,1)S(1)} %copy-done.2) | data formatting | bytes 331776 | tf_op args[5]
  29.0 0.9 %select_n.33.q_ref = bf16[192,256]{1,0:T(8,128)(2,1)} reshape(bf16[3,2,2,8,2,8,32]{6,5,4,3,2,1,0:T(8,128)(2,1)S(1)} %broadcast_select_fusion) | data formatting | bytes 196608 | tf_op jit(solution)/shard_map/jit(_where)/select_n | solution.py:86
  29.9 0.7 tile.18.b_ref
  30.6 0.7 reshape_tile.4.first_bias_ref
  31.3 20.7 %shard_map.104 = bf16[2560,256]{1,0:T(8,128)(2,1)} custom-call(bf16[2560,192]{1,0:T(8,128)(2,1)} %reshape.88.x_ref, bf16[192,256]{1,0:T(8,128)(2,1)} %select_n.33.q_ref, f32[1,256]{1,0:T(1,128)} %reshape_tile.4.first_bias_ref, bf16[3,27,32,32]{3,2,1,0:T(8,128)(2,1)} %bitcast.51, f32[3,1,256]{2,1,0:T(1,128)} %tile.18.b_ref), custom_call_target="tpu_custom_call" | custom-call | tf_op jit(solution)/shard_map/pallas_call | solution.py:93
  52.0 1.6 %copy.28 = f32[2560,256]{0,1:T(8,128)S(1)} copy(bf16[2560,256]{1,0:T(8,128)(2,1)} %shard_map.104) | data formatting | bytes 3932160 | tf_op jit(solution)/shard_map/convert_element_type | solution.py:132
  53.6 2.9 %reshape.94 = f32[40,64,8,32]{1,0,3,2:T(8,128)} reshape(f32[2560,256]{0,1:T(8,128)S(1)} %copy.28) | data formatting | bytes 5242880 | tf_op jit(solution)/shard_map/convert_element_type | solution.py:132
  56.5 1.3 %dynamic_slice.3 = s32[1,1]{0,1:T(1,128)} dynamic-slice(s32[32,16]{0,1:T(8,128)} %param.11, s32[]{:T(128)S(6)} %select_n.30, s32[]{:T(128)S(6)} %select_n.31), dynamic_slice_sizes={1,1} | dynamic-slice | bytes 12 | tf_op jit(solution)/shard_map/dynamic_slice | solution.py:157
  57.7 0.6 iota_compare_fusion.3
  58.4 0.7 bitcast_select_fusion
  59.1 3.1 %multiply_reduce_fusion = f32[40,32]{0,1:T(8,128)S(1)} fusion(f32[40,64,8,32]{1,0,3,2:T(8,128)} %reshape.94, f32[40,64,8]{1,0,2:T(8,128)S(1)} %copy.30), kind=kLoop, calls=%fused_computation | loop fusion | flops 1309440 | bytes 2708480 | tf_op jit(solution)/shard_map/reduce_sum | solution.py:132
  62.2 1.3 %fusion.11 = (f32[40]{0:T(128)S(1)}, bf16[1,1,40]{2,1,0:T(2,128)(2,1)}) fusion(s32[]{:T(128)} %bitcast, f32[32]{0:T(128)S(1)} %copy-done.6, f32[40,32]{0,1:T(8,128)S(1)} %multiply_reduce_fusion, f32[40]{0:T(128)S(1)} %get-tuple-element.2), kind=kOutput, calls=%fused_computation.26 | convolution fusion | flops 16920 | bytes 5652 | tf_op jit(solution)/shard_map/dot_general | solution.py:134
  63.5 0.2 fusion.2
  63.9 14.6 %all_to_all.5 = f32[16,8,128]{2,1,0:T(8,128)S(1)} all-to-all(f32[16,8,128]{2,1,0:T(8,128)S(1)} %convolution_bitcast_fusion), channel_id=1, replica_groups=mesh['bulk'=32,'seg'=16] {'seg'}, dimensions={0} | all-to-all | bytes 131072 | tf_op jit(solution)/shard_map/all_to_all | solution.py:171
  78.5 0.6 reduce_sum.39
  (23 shorter events, 0.5 us)
Async XLA Ops:
  0.6 62.9 %copy-start = (bf16[32,128]{1,0:T(8,128)(2,1)S(1)}, bf16[32,128]{1,0:T(8,128)(2,1)}, u32[]{:S(2)}) copy-start(bf16[32,128]{1,0:T(8,128)(2,1)} %param.17) | copy-start | bytes 24580
  0.6 4.0 %copy-start.1 = (bf16[1,1,40,2,4096]{4,3,2,1,0:T(2,128)(2,1)S(1)}, bf16[1,1,40,2,4096]{4,3,2,1,0:T(2,128)(2,1)}, u32[]{:S(2)}) copy-start(bf16[1,1,40,2,4096]{4,3,2,1,0:T(2,128)(2,1)} %param.10) | copy-start | bytes 1966084
  0.7 4.4 %copy-start.4 = (f32[4,32]{1,0:T(4,128)S(1)}, f32[4,32]{1,0:T(4,128)}, u32[]{:S(2)}) copy-start(f32[4,32]{1,0:T(4,128)} %param.15) | copy-start | bytes 1540
  21.5 6.2 %copy-start.2 = (bf16[3,27,32,32]{3,2,1,0:T(8,128)(2,1)S(1)}, bf16[3,27,32,32]{3,2,1,0:T(8,128)(2,1)}, u32[]{:S(2)}) copy-start(bf16[3,27,32,32]{3,2,1,0:T(8,128)(2,1)} %param.14) | copy-start | bytes 497668
  21.5 7.4 %copy-start.3 = (bf16[32,24]{0,1:T(8,128)(2,1)S(1)}, bf16[32,24]{0,1:T(8,128)(2,1)}, u32[]{:S(2)}) copy-start(bf16[32,24]{0,1:T(8,128)(2,1)} %param.13) | copy-start | bytes 4612
  53.6 4.8 %copy-start.5 = (s32[1,1,40]{2,1,0:T(1,128)S(1)}, s32[1,1,40]{2,1,0:T(1,128)}, u32[]{:S(2)}) copy-start(s32[1,1,40]{2,1,0:T(1,128)} %param.12) | copy-start | bytes 484
  59.1 3.1 %copy-start.6 = (f32[32]{0:T(128)S(1)}, f32[32]{0:T(128)}, u32[]{:S(2)}) copy-start(f32[32]{0:T(128)} %param.16) | copy-start | bytes 388

commit v4 on v3

--- a/solution.py
+++ b/solution.py
@@ -12,8 +12,10 @@
 PAD_ROWS = 16
 
 
-def conv_kernel(x_ref, q_ref, first_bias_ref, w_ref, b_ref, o_ref, pad_ref, col_ref, band_ref):
-    rows, lanes = o_ref.shape
+def conv_kernel(
+    x_ref, q_ref, first_bias_ref, w_ref, b_ref, pool_ref, weight_ref, pad_ref, col_ref, band_ref
+):
+    rows, lanes = pad_ref.shape[0] - 2 * PAD_ROWS, pad_ref.shape[1]
     side = CS // 2
     channels = w_ref.shape[2]
     edge = PAD_ROWS
@@ -69,10 +71,22 @@
                 ).astype(jnp.bfloat16)
         summed = jnp.dot(col_ref[...], band_ref[layer_index], preferred_element_type=jnp.float32)
         hidden = jnp.maximum(summed + b_ref[layer_index], 0.0).astype(jnp.bfloat16)
-        if layer_index + 1 < LAYERS:
-            pad_ref[edge:edge + rows, :] = hidden.astype(jnp.float32)
-        else:
-            o_ref[...] = hidden
+        pad_ref[edge:edge + rows, :] = hidden.astype(jnp.float32)
+    masks = x_ref[:, 0:128].astype(jnp.float32)
+    overlap = masks * pltpu.roll(masks, 64, 1)
+    over_hi = overlap.astype(jnp.bfloat16)
+    over_lo = (overlap - over_hi.astype(jnp.float32)).astype(jnp.bfloat16)
+    cell = lax.broadcasted_iota(jnp.int32, (128, lanes), 0)
+    z_of_lane = lax.broadcasted_iota(jnp.int32, (128, lanes), 1) // channels
+    gather = ((cell < 64) & ((cell // 2) % side == z_of_lane)).astype(jnp.bfloat16)
+    cell_sum = jnp.dot(over_hi, gather, preferred_element_type=jnp.float32) + jnp.dot(
+        over_lo, gather, preferred_element_type=jnp.float32
+    )
+    boundary = cell_sum * 0.125 + 0.1
+    final = pad_ref[edge:edge + rows, :]
+    pairs = rows // (side * side)
+    pool_ref[...] = jnp.sum((final * boundary).reshape(pairs, side * side, lanes), axis=1)
+    weight_ref[...] = jnp.sum(boundary.reshape(pairs, side * side, lanes), axis=1)
 
 
 def conv_layers(features, patch_weight, conv_weight, conv_bias):
@@ -80,7 +94,9 @@
     side = CS // 2
     channels = conv_weight.shape[2]
     lanes = side * channels
-    per_cell = patch_weight.reshape(channels, 3, 2, 2, 2).transpose(1, 2, 3, 4, 0)
+    per_cell = patch_weight.reshape(channels, 3, 2, 2, 2).transpose(1, 2, 3, 4, 0)[
+        jnp.array([1, 2, 0])
+    ]
     z_in = jnp.arange(side)[:, None, None, None]
     z_out = jnp.arange(side)[None, None, :, None]
     patch_matrix = jnp.where(
@@ -100,8 +116,14 @@
             pl.BlockSpec((LAYERS, 27, channels, channels), lambda i: (0, 0, 0, 0)),
             pl.BlockSpec((LAYERS, 1, lanes), lambda i: (0, 0, 0)),
         ],
-        out_specs=pl.BlockSpec((block_rows, lanes), lambda i: (i, 0)),
-        out_shape=jax.ShapeDtypeStruct((total_rows, lanes), jnp.bfloat16),
+        out_specs=[
+            pl.BlockSpec((BLOCK_PAIRS, lanes), lambda i: (i, 0)),
+            pl.BlockSpec((BLOCK_PAIRS, lanes), lambda i: (i, 0)),
+        ],
+        out_shape=[
+            jax.ShapeDtypeStruct((total_rows // (side * side), lanes), jnp.float32),
+            jax.ShapeDtypeStruct((total_rows // (side * side), lanes), jnp.float32),
+        ],
         scratch_shapes=[
             pltpu.VMEM((block_rows + 2 * PAD_ROWS, lanes), jnp.float32),
             pltpu.VMEM((block_rows, 9 * lanes), jnp.bfloat16),
@@ -120,17 +142,13 @@
     channels = conv_weight.shape[2]
     lanes = side_half * channels
     highest = lax.Precision.HIGHEST
-    stacked = jnp.concatenate([em_rows[:, None, :], mask_rows], axis=1)
+    stacked = jnp.concatenate([mask_rows, em_rows[:, None, :]], axis=1)
     cells = stacked.reshape(rows_here, 3, side_half, 2, side_half, 2 * CS)
     features = cells.transpose(0, 2, 4, 1, 3, 5).reshape(rows_here * side_half * side_half, 12 * CS)
-    hidden = conv_layers(features, patch_weight, conv_weight, conv_bias)
-    hidden = hidden.reshape(rows_here, side_half * side_half, side_half, channels)
-    intersection = mask_rows[:, 0].astype(jnp.float32) * mask_rows[:, 1].astype(jnp.float32)
-    intersection = intersection.reshape(rows_here, side_half, 2, side_half, 2, side_half, 2)
-    boundary = jnp.mean(intersection, axis=(2, 4, 6))
-    boundary = boundary.reshape(rows_here, side_half * side_half, side_half) + 0.1
-    pooled = jnp.sum(hidden.astype(jnp.float32) * boundary[..., None], axis=(1, 2))
-    pooled = pooled / jnp.sum(boundary, axis=(1, 2))[:, None]
+    pool_sum, weight_sum = conv_layers(features, patch_weight, conv_weight, conv_bias)
+    pooled = jnp.sum(pool_sum.reshape(rows_here, side_half, channels), axis=1)
+    total_weight = jnp.sum(weight_sum.reshape(rows_here, side_half, channels)[:, :, 0], axis=1)
+    pooled = pooled / total_weight[:, None]
     logits = jnp.dot(pooled, score_weight, precision=highest)
     scores = jax.nn.sigmoid(logits).astype(jnp.bfloat16)
     embedded = jnp.tanh(jnp.dot(pooled, embed_weight.astype(jnp.float32), precision=highest))

time: 79.7 us -> 70.5 us (0.88)
  other arithmetic: 10.5 us -> 4.62 us
  local copies, waits for them, and re-layouts: 30.9 us -> 26.9 us
    convert_element_type x2 -> x0, local copies, waits for them, and re-layouts: 4.48 us -> none  [run_network(): hidden.astype(jnp.float32) * boundary[..., None]]
    reduce_sum x3 -> x2, other arithmetic: 4.63 us -> 0.43 us  [the longest x1 0.38 us: run_network(): jnp.sum(weight_sum.reshape(rows_here, side_half, channels)[:, :, 0], axis=1)]
    unnamed x17 -> x14, local copies, waits for them, and re-layouts: 5.54 us -> 2.57 us
    mul x1 -> x0, other arithmetic: 1.75 us -> none  [run_network(): mask_rows[:, 0].astype(jnp.float32) * mask_rows[:, 1].astype(jnp.float32)]
    reshape x0 -> x2, local copies, waits for them, and re-layouts: none -> 1.74 us  [the longest x1 0.87 us: run_network(): weight_sum.reshape(rows_here, side_half, channels)[:, :, 0]]
where the time goes in v4:
time: 70.5 us; the launch traced here: 69.9 us
  local copies, waits for them, and re-layouts  26.9 us (38%)
  Pallas kernels  21.2 us (30%)
  blocking collectives  14.6 us (21%)
  other arithmetic  4.62 us (7%)
  matrix products  1.76 us (2%)
  between operations  0.76 us (1%)
    pallas_call x1, Pallas kernels, conv_layers(): pl.pallas_call(conv_kernel, grid=(total_rows // block_rows,), in_specs=[p...  21.2 us
    all_to_all x1, blocking collectives, per_device(): arrived = lax.all_to_all(partial_value, 'seg', 0, 0, tiled=True)  14.6 us
    reshape x1, local copies, waits for them, and re-layouts, run_network(): cells.transpose(0, 2, 4, 1, 3, 5)  6.22 us
    transpose x1, local copies, waits for them, and re-layouts, run_network(): cells.transpose(0, 2, 4, 1, 3, 5)  5.99 us
    concatenate x2, local copies, waits for them, and re-layouts, run_network(): stacked = jnp.concatenate([mask_rows, em_rows[:, None, :]], axis=1)  4.94 us
    unnamed x14, local copies, waits for them, and re-layouts  2.57 us
    transpose x1, other arithmetic, run_network(): cells.transpose(0, 2, 4, 1, 3, 5)  2.16 us

profile of v4, /device:TPU:2, one launch (start us, length us, event | category | flops | bytes accessed | tf_op | source)
XLA Modules:
  0.0 69.9 jit_solution(8267102238633393277)
XLA Ops:
  0.7 0.7 slice.10
  1.3 0.7 slice_bitcast_fusion
  2.0 1.5 %copy.15 = bf16[1,1,40,2,4096]{4,2,3,1,0:T(8,128)(2,1)S(1)} copy(bf16[1,1,40,2,4096]{4,3,2,1,0:T(2,128)(2,1)} %param.11) | data formatting | bytes 1310720 | tf_op args[1]
  3.5 2.1 %concatenate.8 = bf16[40,2,8,2,8,32]{5,4,3,2,0,1:T(8,128)(2,1)S(1)} reshape(bf16[1,1,40,2,4096]{4,2,3,1,0:T(8,128)(2,1)S(1)} %copy.15) | data formatting | bytes 1310720 | tf_op jit(solution)/shard_map/concatenate | solution.py:145
  5.6 2.9 %concatenate.9 = bf16[40,1,8,2,8,32]{5,4,3,2,0,1:T(8,128)(2,1)} reshape(bf16[1,1,40,4096]{3,2,1,0:T(8,128)(2,1)} %param.10) | data formatting | bytes 655360 | tf_op jit(solution)/shard_map/concatenate | solution.py:145
  8.4 2.2 %maximum_bitcast_fusion = bf16[40,8,8,3,2,32]{5,2,4,1,0,3:T(8,128)(2,1)S(1)} fusion(bf16[40,1,8,2,8,32]{5,4,3,2,0,1:T(8,128)(2,1)} %concatenate.9, bf16[40,2,8,2,8,32]{5,4,3,2,0,1:T(8,128)(2,1)S(1)} %concatenate.8), kind=kLoop, calls=%fused_computation.1 | loop fusion | flops 491520 | bytes 1966080 | tf_op jit(solution)/shard_map/transpose | solution.py:147
  10.6 6.0 %copy.16 = bf16[40,8,8,3,2,32]{5,4,3,2,1,0:T(2,128)(2,1)} copy(bf16[40,8,8,3,2,32]{5,2,4,1,0,3:T(8,128)(2,1)S(1)} %maximum_bitcast_fusion) | data formatting | bytes 1966080 | tf_op jit(solution)/shard_map/transpose | solution.py:147
  16.6 6.2 %reshape.71.x_ref = bf16[2560,192]{1,0:T(8,128)(2,1)} reshape(bf16[40,8,8,3,2,32]{5,4,3,2,1,0:T(2,128)(2,1)} %copy.16) | data formatting | bytes 1966080 | tf_op jit(solution)/shard_map/reshape | solution.py:147
  22.8 1.1 %copy.17 = bf16[3,27,32,32]{2,3,1,0:T(8,128)(2,1)} copy(bf16[3,27,32,32]{3,2,1,0:T(8,128)(2,1)S(1)} %copy-done.1) | data formatting | bytes 331776 | tf_op args[5]
  24.0 0.6 gather_fusion
  24.6 0.9 %select_n.37.q_ref = bf16[192,256]{1,0:T(8,128)(2,1)} reshape(bf16[3,2,2,8,2,8,32]{6,5,4,3,2,1,0:T(8,128)(2,1)S(1)} %broadcast_select_fusion) | data formatting | bytes 196608 | tf_op jit(solution)/shard_map/jit(_where)/select_n | solution.py:102
  25.6 0.7 tile.18.b_ref
  26.2 0.6 reshape_tile.4.first_bias_ref
  26.9 21.2 %shard_map.113 = (f32[40,256]{1,0:T(8,128)}, f32[40,256]{1,0:T(8,128)}) custom-call(bf16[2560,192]{1,0:T(8,128)(2,1)} %reshape.71.x_ref, bf16[192,256]{1,0:T(8,128)(2,1)} %select_n.37.q_ref, f32[1,256]{1,0:T(1,128)} %reshape_tile.4.first_bias_ref, bf16[3,27,32,32]{3,2,1,0:T(8,128)(2,1)} %bitcast.44, f32[3,1,256]{2,1,0:T(1,128)} %tile.18.b_ref), custom_call_target="tpu_custom_call" | custom-call | tf_op jit(solution)/shard_map/pallas_call | solution.py:109
  48.1 0.9 %reshape.73 = f32[40,8,32]{2,1,0:T(8,128)S(1)} reshape(f32[40,256]{1,0:T(8,128)} %get-tuple-element.4) | data formatting | bytes 81920 | tf_op jit(solution)/shard_map/reshape | solution.py:149
  49.0 0.9 %reshape.74 = f32[40,8,32]{2,1,0:T(8,128)S(1)} reshape(f32[40,256]{1,0:T(8,128)} %get-tuple-element.5) | data formatting | bytes 81920 | tf_op jit(solution)/shard_map/reshape | solution.py:150
  49.9 0.4 slice_reduce_fusion
  50.2 1.3 %dynamic_slice.3 = s32[1,1]{0,1:T(1,128)} dynamic-slice(s32[32,16]{0,1:T(8,128)} %param.12, s32[]{:T(128)S(6)} %select_n.33, s32[]{:T(128)S(6)} %select_n.34), dynamic_slice_sizes={1,1} | dynamic-slice | bytes 12 | tf_op jit(solution)/shard_map/dynamic_slice | solution.py:175
  51.5 0.6 iota_compare_fusion.3
  52.2 0.7 bitcast_select_fusion
  52.9 1.4 %fusion.10 = (f32[40]{0:T(128)S(1)}, bf16[1,1,40]{2,1,0:T(2,128)(2,1)}) fusion(s32[]{:T(128)} %bitcast, f32[32]{0:T(128)S(1)} %copy-done.5, f32[40,32]{1,0:T(8,128)S(1)} %reduce_sum.27, f32[40]{0:T(128)S(1)} %slice_reduce_fusion), kind=kOutput, calls=%fused_computation.25 | convolution fusion | flops 16920 | bytes 5652 | tf_op jit(solution)/shard_map/dot_general | solution.py:152
  54.3 0.2 fusion.2
  54.7 14.6 %all_to_all.5 = f32[16,8,128]{2,1,0:T(8,128)S(1)} all-to-all(f32[16,8,128]{2,1,0:T(8,128)S(1)} %convolution_bitcast_fusion), channel_id=1, replica_groups=mesh['bulk'=32,'seg'=16] {'seg'}, dimensions={0} | all-to-all | bytes 131072 | tf_op jit(solution)/shard_map/all_to_all | solution.py:189
  69.3 0.6 reduce_sum.29
  (19 shorter events, 0.3 us)
Async XLA Ops:
  0.6 53.7 %copy-start = (bf16[32,128]{1,0:T(8,128)(2,1)S(1)}, bf16[32,128]{1,0:T(8,128)(2,1)}, u32[]{:S(2)}) copy-start(bf16[32,128]{1,0:T(8,128)(2,1)} %param.18) | copy-start | bytes 24580
  16.6 6.3 %copy-start.1 = (bf16[3,27,32,32]{3,2,1,0:T(8,128)(2,1)S(1)}, bf16[3,27,32,32]{3,2,1,0:T(8,128)(2,1)}, u32[]{:S(2)}) copy-start(bf16[3,27,32,32]{3,2,1,0:T(8,128)(2,1)} %param.15) | copy-start | bytes 497668
  16.6 7.3 %copy-start.3 = (s32[3]{0:T(128)S(1)}, s32[3]{0:T(128)}, u32[]{:S(2)}) copy-start(s32[3]{0:T(128)} %constant.36) | copy-start | bytes 40
  16.6 7.4 %copy-start.2 = (bf16[32,24]{0,1:T(8,128)(2,1)S(1)}, bf16[32,24]{0,1:T(8,128)(2,1)}, u32[]{:S(2)}) copy-start(bf16[32,24]{0,1:T(8,128)(2,1)} %param.14) | copy-start | bytes 4612
  16.6 35.6 %copy-start.4 = (s32[1,1,40]{2,1,0:T(1,128)S(1)}, s32[1,1,40]{2,1,0:T(1,128)}, u32[]{:S(2)}) copy-start(s32[1,1,40]{2,1,0:T(1,128)} %param.13) | copy-start | bytes 484
  16.6 36.3 %copy-start.5 = (f32[32]{0:T(128)S(1)}, f32[32]{0:T(128)}, u32[]{:S(2)}) copy-start(f32[32]{0:T(128)} %param.17) | copy-start | bytes 388

commit v5 on v4

--- a/solution.py
+++ b/solution.py
@@ -144,7 +144,14 @@
     highest = lax.Precision.HIGHEST
     stacked = jnp.concatenate([mask_rows, em_rows[:, None, :]], axis=1)
     cells = stacked.reshape(rows_here, 3, side_half, 2, side_half, 2 * CS)
-    features = cells.transpose(0, 2, 4, 1, 3, 5).reshape(rows_here * side_half * side_half, 12 * CS)
+    features = jnp.concatenate(
+        [
+            cells[:, channel, :, half].reshape(rows_here * side_half * side_half, 2 * CS)
+            for channel in range(3)
+            for half in range(2)
+        ],
+        axis=1,
+    )
     pool_sum, weight_sum = conv_layers(features, patch_weight, conv_weight, conv_bias)
     pooled = jnp.sum(pool_sum.reshape(rows_here, side_half, channels), axis=1)
     total_weight = jnp.sum(weight_sum.reshape(rows_here, side_half, channels)[:, :, 0], axis=1)

time: 70.5 us -> 65.8 us (0.933)
  local copies, waits for them, and re-layouts: 26.9 us -> 23.6 us
  other arithmetic: 4.62 us -> 3.2 us
    reshape x1 -> x0, local copies, waits for them, and re-layouts: 6.22 us -> none  [run_network(): cells.transpose(0, 2, 4, 1, 3, 5)]
    transpose x1 -> x0, local copies, waits for them, and re-layouts: 5.99 us -> none  [run_network(): cells.transpose(0, 2, 4, 1, 3, 5)]
    concatenate x0 -> x1, local copies, waits for them, and re-layouts: none -> 4.46 us  [run_network(): jnp.concatenate([cells[:, channel, :, half].reshape(rows_here * side_half...]
    slice x0 -> x2, local copies, waits for them, and re-layouts: none -> 2.99 us  [run_network(): cells[:, channel, :, half]]
    transpose x1 -> x0, other arithmetic: 2.16 us -> none  [run_network(): cells.transpose(0, 2, 4, 1, 3, 5)]
    unnamed x14 -> x18, local copies, waits for them, and re-layouts: 2.57 us -> 3.84 us
    select_n x1, local copies, waits for them, and re-layouts: 0.92 us -> 1.94 us  [conv_layers(): jnp.where(z_in == z_out, per_cell[:, :, :, None, :, None, :], 0)]
    concatenate x2, local copies, waits for them, and re-layouts: 4.94 us -> 4.12 us  [run_network(): stacked = jnp.concatenate([mask_rows, em_rows[:, None, :]], axis=1)]
where the time goes in v5:
time: 65.8 us; the launch traced here: 65.2 us
  local copies, waits for them, and re-layouts  23.6 us (36%)
  Pallas kernels  21.2 us (32%)
  blocking collectives  14.6 us (22%)
  other arithmetic  3.2 us (5%)
  matrix products  1.76 us (3%)
  between operations  0.77 us (1%)
    pallas_call x1, Pallas kernels, conv_layers(): pl.pallas_call(conv_kernel, grid=(total_rows // block_rows,), in_specs=[p...  21.2 us
    all_to_all x1, blocking collectives, per_device(): arrived = lax.all_to_all(partial_value, 'seg', 0, 0, tiled=True)  14.6 us
    concatenate x1, local copies, waits for them, and re-layouts, run_network(): jnp.concatenate([cells[:, channel, :, half].reshape(rows_here * side_half...  4.46 us
    concatenate x2, local copies, waits for them, and re-layouts, run_network(): stacked = jnp.concatenate([mask_rows, em_rows[:, None, :]], axis=1)  4.12 us
    unnamed x18, local copies, waits for them, and re-layouts  3.84 us
    slice x2, local copies, waits for them, and re-layouts, run_network(): cells[:, channel, :, half]  2.99 us
    select_n x1, local copies, waits for them, and re-layouts, conv_layers(): jnp.where(z_in == z_out, per_cell[:, :, :, None, :, None, :], 0)  1.94 us
    dot_general x1, matrix products, run_network(): logits = jnp.dot(pooled, score_weight, precision=highest)  1.4 us

profile of v5, /device:TPU:2, one launch (start us, length us, event | category | flops | bytes accessed | tf_op | source)
XLA Modules:
  0.0 65.2 jit_solution(448817077787714568)
XLA Ops:
  0.7 0.7 %slice.40 = f32[3,32]{1,0:T(4,128)S(1)} slice(f32[4,32]{1,0:T(4,128)} %param.16), slice={[1:4], [0:32]} | slice | bytes 768 | tf_op jit(solution)/shard_map/slice | solution.py:107
  1.3 0.7 %slice_bitcast_fusion = f32[32]{0:T(128)S(1)} fusion(f32[4,32]{1,0:T(4,128)} %param.16), kind=kLoop, calls=%fused_computation.22 | loop fusion | bytes 256 | tf_op jit(solution)/shard_map/tile | solution.py:105
  2.0 1.5 %copy.19 = bf16[1,1,40,2,4096]{4,2,3,1,0:T(8,128)(2,1)S(1)} copy(bf16[1,1,40,2,4096]{4,3,2,1,0:T(2,128)(2,1)} %param.11) | data formatting | bytes 1310720 | tf_op args[1]
  3.5 2.1 %concatenate.9 = bf16[40,2,8,2,8,32]{5,4,3,2,0,1:T(8,128)(2,1)S(1)} reshape(bf16[1,1,40,2,4096]{4,2,3,1,0:T(8,128)(2,1)S(1)} %copy.19) | data formatting | bytes 1310720 | tf_op jit(solution)/shard_map/concatenate | solution.py:145
  5.6 1.8 %fusion.10 = (bf16[40,1,8,1,8,32]{5,4,3,2,0,1:T(8,128)(2,1)S(1)}, bf16[40,1,8,1,8,32]{5,4,3,2,0,1:T(8,128)(2,1)}, bf16[40,1,8,1,8,32]{5,4,3,2,0,1:T(8,128)(2,1)}, bf16[40,1,8,1,8,32]{5,4,3,2,0,1:T(8,128)(2,1)}) fusion(bf16[40,2,8,2,8,32]{5,4,3,2,0,1:T(8,128)(2,1)S(1)} %concatenate.9), kind=kLoop, calls=%fused_computation.24 | loop fusion | bytes 1310720 | tf_op jit(solution)/shard_map/slice | solution.py:149
  7.3 2.0 %concatenate.10 = bf16[40,1,8,2,8,32]{5,4,3,2,0,1:T(8,128)(2,1)S(1)} reshape(bf16[1,1,40,4096]{3,2,1,0:T(8,128)(2,1)} %param.10) | data formatting | bytes 655360 | tf_op jit(solution)/shard_map/concatenate | solution.py:145
  9.4 1.2 %fusion.11 = (bf16[40,1,8,1,8,32]{5,4,3,2,0,1:T(8,128)(2,1)S(1)}, bf16[40,1,8,1,8,32]{5,4,3,2,0,1:T(8,128)(2,1)}) fusion(bf16[40,1,8,2,8,32]{5,4,3,2,0,1:T(8,128)(2,1)S(1)} %concatenate.10), kind=kLoop, calls=%fused_computation.25 | loop fusion | bytes 655360 | tf_op jit(solution)/shard_map/slice | solution.py:149
  10.6 2.4 %copy.20 = bf16[3,27,32,32]{2,3,1,0:T(8,128)(2,1)} copy(bf16[3,27,32,32]{3,2,1,0:T(8,128)(2,1)} %param.15) | data formatting | bytes 331776 | tf_op args[5]
  13.0 0.6 gather_fusion
  13.6 0.9 %broadcast_select_fusion = bf16[3,2,2,8,2,8,32]{6,5,4,3,2,1,0:T(8,128)(2,1)} fusion(pred[8,8]{1,0:T(8,128)(4,1)S(1)} %iota_compare_fusion.2, bf16[3,2,2,2,32]{4,3,2,1,0:T(2,128)(2,1)S(1)} %gather_fusion), kind=kLoop, calls=%fused_computation.12 | loop fusion | flops 49152 | bytes 99904 | tf_op jit(solution)/shard_map/jit(_where)/select_n | solution.py:102
  14.4 1.9 %select_n.37.q_ref = bf16[192,256]{1,0:T(8,128)(2,1)} reshape(bf16[3,2,2,8,2,8,32]{6,5,4,3,2,1,0:T(8,128)(2,1)} %broadcast_select_fusion) | data formatting | bytes 196608 | tf_op jit(solution)/shard_map/jit(_where)/select_n | solution.py:102
  16.4 0.7 %tile.18.b_ref = f32[3,1,256]{2,1,0:T(1,128)} reshape(f32[3,8,32]{2,1,0:T(8,128)S(1)} %tile.17) | data formatting | bytes 6144 | tf_op jit(solution)/shard_map/tile | solution.py:107
  17.1 0.6 reshape_tile.4.first_bias_ref
  17.7 4.5 %concatenate.11.x_ref = bf16[2560,192]{1,0:T(8,128)(2,1)} concatenate(bf16[2560,32]{1,0:T(8,128)(2,1)S(1)} %bitcast.52, bf16[2560,32]{1,0:T(8,128)(2,1)S(1)} %bitcast.51, bf16[2560,32]{1,0:T(8,128)(2,1)S(1)} %bitcast.50, bf16[2560,32]{1,0:T(8,128)(2,1)S(1)} %bitcast.49, bf16[2560,32]{1,0:T(8,128)(2,1)} %bitcast.54, bf16[2560,32]{1,0:T(8,128)(2,1)S(1)} %bitcast.53), dimensions={1} | concatenate | bytes 1966080 | tf_op jit(solution)/shard_map/concatenate | solution.py:147
  22.2 21.2 %shard_map.113 = (f32[40,256]{1,0:T(8,128)}, f32[40,256]{1,0:T(8,128)}) custom-call(bf16[2560,192]{1,0:T(8,128)(2,1)} %concatenate.11.x_ref, bf16[192,256]{1,0:T(8,128)(2,1)} %select_n.37.q_ref, f32[1,256]{1,0:T(1,128)} %reshape_tile.4.first_bias_ref, bf16[3,27,32,32]{3,2,1,0:T(8,128)(2,1)} %bitcast.48, f32[3,1,256]{2,1,0:T(1,128)} %tile.18.b_ref), custom_call_target="tpu_custom_call" | custom-call | tf_op jit(solution)/shard_map/pallas_call | solution.py:109
  43.4 0.9 %reshape.69 = f32[40,8,32]{2,1,0:T(8,128)S(1)} reshape(f32[40,256]{1,0:T(8,128)} %get-tuple-element.4) | data formatting | bytes 81920 | tf_op jit(solution)/shard_map/reshape | solution.py:156
  44.3 0.9 %reshape.70 = f32[40,8,32]{2,1,0:T(8,128)S(1)} reshape(f32[40,256]{1,0:T(8,128)} %get-tuple-element.5) | data formatting | bytes 81920 | tf_op jit(solution)/shard_map/reshape | solution.py:157
  45.1 0.4 slice_reduce_fusion
  45.5 1.3 %dynamic_slice.3 = s32[1,1]{0,1:T(1,128)} dynamic-slice(s32[32,16]{0,1:T(8,128)} %param.12, s32[]{:T(128)S(6)} %select_n.33, s32[]{:T(128)S(6)} %select_n.34), dynamic_slice_sizes={1,1} | dynamic-slice | bytes 12 | tf_op jit(solution)/shard_map/dynamic_slice | solution.py:182
  46.8 0.6 iota_compare_fusion.3
  47.5 0.7 bitcast_select_fusion
  48.2 1.4 %fusion.12 = (f32[40]{0:T(128)S(1)}, bf16[1,1,40]{2,1,0:T(2,128)(2,1)}) fusion(s32[]{:T(128)} %bitcast, f32[32]{0:T(128)S(1)} %copy-done.7, f32[40,32]{1,0:T(8,128)S(1)} %reduce_sum.27, f32[40]{0:T(128)S(1)} %slice_reduce_fusion), kind=kOutput, calls=%fused_computation.26 | convolution fusion | flops 16920 | bytes 5652 | tf_op jit(solution)/shard_map/dot_general | solution.py:159
  50.0 14.6 %all_to_all.5 = f32[16,8,128]{2,1,0:T(8,128)S(1)} all-to-all(f32[16,8,128]{2,1,0:T(8,128)S(1)} %convolution_bitcast_fusion), channel_id=1, replica_groups=mesh['bulk'=32,'seg'=16] {'seg'}, dimensions={0} | all-to-all | bytes 131072 | tf_op jit(solution)/shard_map/all_to_all | solution.py:196
  64.6 0.6 reduce_sum.29
  (23 shorter events, 0.5 us)
Async XLA Ops:
  0.6 49.0 %copy-start = (bf16[32,128]{1,0:T(8,128)(2,1)S(1)}, bf16[32,128]{1,0:T(8,128)(2,1)}, u32[]{:S(2)}) copy-start(bf16[32,128]{1,0:T(8,128)(2,1)} %param.18) | copy-start | bytes 24580
  9.4 3.6 %copy-start.5 = (s32[3]{0:T(128)S(1)}, s32[3]{0:T(128)}, u32[]{:S(2)}) copy-start(s32[3]{0:T(128)} %constant.36) | copy-start | bytes 40
  9.4 3.6 %copy-start.4 = (bf16[32,24]{0,1:T(8,128)(2,1)S(1)}, bf16[32,24]{0,1:T(8,128)(2,1)}, u32[]{:S(2)}) copy-start(bf16[32,24]{0,1:T(8,128)(2,1)} %param.14) | copy-start | bytes 4612
  10.6 7.0 %copy-start.1 = (bf16[40,1,8,1,8,32]{5,4,3,2,0,1:T(8,128)(2,1)S(1)}, bf16[40,1,8,1,8,32]{5,4,3,2,0,1:T(8,128)(2,1)}, u32[]{:S(2)}) copy-start(bf16[40,1,8,1,8,32]{5,4,3,2,0,1:T(8,128)(2,1)} %get-tuple-element.7) | copy-start | bytes 491524
  10.6 7.0 %copy-start.2 = (bf16[40,1,8,1,8,32]{5,4,3,2,0,1:T(8,128)(2,1)S(1)}, bf16[40,1,8,1,8,32]{5,4,3,2,0,1:T(8,128)(2,1)}, u32[]{:S(2)}) copy-start(bf16[40,1,8,1,8,32]{5,4,3,2,0,1:T(8,128)(2,1)} %get-tuple-element.8) | copy-start | bytes 491524
  10.6 7.0 %copy-start.3 = (bf16[40,1,8,1,8,32]{5,4,3,2,0,1:T(8,128)(2,1)S(1)}, bf16[40,1,8,1,8,32]{5,4,3,2,0,1:T(8,128)(2,1)}, u32[]{:S(2)}) copy-start(bf16[40,1,8,1,8,32]{5,4,3,2,0,1:T(8,128)(2,1)} %get-tuple-element.9) | copy-start | bytes 491524
  22.2 25.3 %copy-start.6 = (s32[1,1,40]{2,1,0:T(1,128)S(1)}, s32[1,1,40]{2,1,0:T(1,128)}, u32[]{:S(2)}) copy-start(s32[1,1,40]{2,1,0:T(1,128)} %param.13) | copy-start | bytes 484
  22.2 26.0 %copy-start.7 = (f32[32]{0:T(128)S(1)}, f32[32]{0:T(128)}, u32[]{:S(2)}) copy-start(f32[32]{0:T(128)} %param.17) | copy-start | bytes 388

commit v6 on v5

--- a/solution.py
+++ b/solution.py
@@ -54,7 +54,7 @@
     first = jnp.dot(x_ref[...], q_ref[...], preferred_element_type=jnp.float32)
     first = jnp.maximum(first + first_bias_ref[...], 0.0).astype(jnp.bfloat16)
     pad_ref[edge:edge + rows, :] = first.astype(jnp.float32)
-    row_id = lax.broadcasted_iota(jnp.int32, (rows, lanes), 0)
+    row_id = lax.broadcasted_iota(jnp.int32, (rows, 1), 0)
     y_pos = row_id % side
     x_pos = (row_id // side) % side
     for layer_index in range(LAYERS):

time: 65.8 us -> 65.7 us (level)
  no operation moved by 1% of the time
where the time goes in v6:
time: 65.7 us; the launch traced here: 65.1 us
  local copies, waits for them, and re-layouts  23.6 us (36%)
  Pallas kernels  21.1 us (32%)
  blocking collectives  14.6 us (22%)
  other arithmetic  3.2 us (5%)
  matrix products  1.76 us (3%)
  between operations  0.77 us (1%)
    pallas_call x1, Pallas kernels, conv_layers(): pl.pallas_call(conv_kernel, grid=(total_rows // block_rows,), in_specs=[p...  21.1 us
    all_to_all x1, blocking collectives, per_device(): arrived = lax.all_to_all(partial_value, 'seg', 0, 0, tiled=True)  14.6 us
    concatenate x1, local copies, waits for them, and re-layouts, run_network(): jnp.concatenate([cells[:, channel, :, half].reshape(rows_here * side_half...  4.46 us
    concatenate x2, local copies, waits for them, and re-layouts, run_network(): stacked = jnp.concatenate([mask_rows, em_rows[:, None, :]], axis=1)  4.12 us
    unnamed x18, local copies, waits for them, and re-layouts  3.84 us
    slice x2, local copies, waits for them, and re-layouts, run_network(): cells[:, channel, :, half]  2.99 us
    select_n x1, local copies, waits for them, and re-layouts, conv_layers(): jnp.where(z_in == z_out, per_cell[:, :, :, None, :, None, :], 0)  1.94 us
    dot_general x1, matrix products, run_network(): logits = jnp.dot(pooled, score_weight, precision=highest)  1.4 us

profile of v6, /device:TPU:2, one launch (start us, length us, event | category | flops | bytes accessed | tf_op | source)
XLA Modules:
  0.0 65.1 jit_solution(13439489869905287058)
XLA Ops:
  0.7 0.7 %slice.40 = f32[3,32]{1,0:T(4,128)S(1)} slice(f32[4,32]{1,0:T(4,128)} %param.16), slice={[1:4], [0:32]} | slice | bytes 768 | tf_op jit(solution)/shard_map/slice | solution.py:107
  1.3 0.7 %slice_bitcast_fusion = f32[32]{0:T(128)S(1)} fusion(f32[4,32]{1,0:T(4,128)} %param.16), kind=kLoop, calls=%fused_computation.22 | loop fusion | bytes 256 | tf_op jit(solution)/shard_map/tile | solution.py:105
  2.0 1.5 %copy.19 = bf16[1,1,40,2,4096]{4,2,3,1,0:T(8,128)(2,1)S(1)} copy(bf16[1,1,40,2,4096]{4,3,2,1,0:T(2,128)(2,1)} %param.11) | data formatting | bytes 1310720 | tf_op args[1]
  3.5 2.1 %concatenate.9 = bf16[40,2,8,2,8,32]{5,4,3,2,0,1:T(8,128)(2,1)S(1)} reshape(bf16[1,1,40,2,4096]{4,2,3,1,0:T(8,128)(2,1)S(1)} %copy.19) | data formatting | bytes 1310720 | tf_op jit(solution)/shard_map/concatenate | solution.py:145
  5.6 1.8 %fusion.10 = (bf16[40,1,8,1,8,32]{5,4,3,2,0,1:T(8,128)(2,1)S(1)}, bf16[40,1,8,1,8,32]{5,4,3,2,0,1:T(8,128)(2,1)}, bf16[40,1,8,1,8,32]{5,4,3,2,0,1:T(8,128)(2,1)}, bf16[40,1,8,1,8,32]{5,4,3,2,0,1:T(8,128)(2,1)}) fusion(bf16[40,2,8,2,8,32]{5,4,3,2,0,1:T(8,128)(2,1)S(1)} %concatenate.9), kind=kLoop, calls=%fused_computation.24 | loop fusion | bytes 1310720 | tf_op jit(solution)/shard_map/slice | solution.py:149
  7.3 2.0 %concatenate.10 = bf16[40,1,8,2,8,32]{5,4,3,2,0,1:T(8,128)(2,1)S(1)} reshape(bf16[1,1,40,4096]{3,2,1,0:T(8,128)(2,1)} %param.10) | data formatting | bytes 655360 | tf_op jit(solution)/shard_map/concatenate | solution.py:145
  9.4 1.2 %fusion.11 = (bf16[40,1,8,1,8,32]{5,4,3,2,0,1:T(8,128)(2,1)S(1)}, bf16[40,1,8,1,8,32]{5,4,3,2,0,1:T(8,128)(2,1)}) fusion(bf16[40,1,8,2,8,32]{5,4,3,2,0,1:T(8,128)(2,1)S(1)} %concatenate.10), kind=kLoop, calls=%fused_computation.25 | loop fusion | bytes 655360 | tf_op jit(solution)/shard_map/slice | solution.py:149
  10.6 2.4 %copy.20 = bf16[3,27,32,32]{2,3,1,0:T(8,128)(2,1)} copy(bf16[3,27,32,32]{3,2,1,0:T(8,128)(2,1)} %param.15) | data formatting | bytes 331776 | tf_op args[5]
  13.0 0.6 gather_fusion
  13.6 0.9 %broadcast_select_fusion = bf16[3,2,2,8,2,8,32]{6,5,4,3,2,1,0:T(8,128)(2,1)} fusion(pred[8,8]{1,0:T(8,128)(4,1)S(1)} %iota_compare_fusion.2, bf16[3,2,2,2,32]{4,3,2,1,0:T(2,128)(2,1)S(1)} %gather_fusion), kind=kLoop, calls=%fused_computation.12 | loop fusion | flops 49152 | bytes 99904 | tf_op jit(solution)/shard_map/jit(_where)/select_n | solution.py:102
  14.4 1.9 %select_n.37.q_ref = bf16[192,256]{1,0:T(8,128)(2,1)} reshape(bf16[3,2,2,8,2,8,32]{6,5,4,3,2,1,0:T(8,128)(2,1)} %broadcast_select_fusion) | data formatting | bytes 196608 | tf_op jit(solution)/shard_map/jit(_where)/select_n | solution.py:102
  16.4 0.7 %tile.18.b_ref = f32[3,1,256]{2,1,0:T(1,128)} reshape(f32[3,8,32]{2,1,0:T(8,128)S(1)} %tile.17) | data formatting | bytes 6144 | tf_op jit(solution)/shard_map/tile | solution.py:107
  17.1 0.6 reshape_tile.4.first_bias_ref
  17.7 4.5 %concatenate.11.x_ref = bf16[2560,192]{1,0:T(8,128)(2,1)} concatenate(bf16[2560,32]{1,0:T(8,128)(2,1)S(1)} %bitcast.52, bf16[2560,32]{1,0:T(8,128)(2,1)S(1)} %bitcast.51, bf16[2560,32]{1,0:T(8,128)(2,1)S(1)} %bitcast.50, bf16[2560,32]{1,0:T(8,128)(2,1)S(1)} %bitcast.49, bf16[2560,32]{1,0:T(8,128)(2,1)} %bitcast.54, bf16[2560,32]{1,0:T(8,128)(2,1)S(1)} %bitcast.53), dimensions={1} | concatenate | bytes 1966080 | tf_op jit(solution)/shard_map/concatenate | solution.py:147
  22.2 21.1 %shard_map.113 = (f32[40,256]{1,0:T(8,128)}, f32[40,256]{1,0:T(8,128)}) custom-call(bf16[2560,192]{1,0:T(8,128)(2,1)} %concatenate.11.x_ref, bf16[192,256]{1,0:T(8,128)(2,1)} %select_n.37.q_ref, f32[1,256]{1,0:T(1,128)} %reshape_tile.4.first_bias_ref, bf16[3,27,32,32]{3,2,1,0:T(8,128)(2,1)} %bitcast.48, f32[3,1,256]{2,1,0:T(1,128)} %tile.18.b_ref), custom_call_target="tpu_custom_call" | custom-call | tf_op jit(solution)/shard_map/pallas_call | solution.py:109
  43.3 0.9 %reshape.69 = f32[40,8,32]{2,1,0:T(8,128)S(1)} reshape(f32[40,256]{1,0:T(8,128)} %get-tuple-element.4) | data formatting | bytes 81920 | tf_op jit(solution)/shard_map/reshape | solution.py:156
  44.2 0.9 %reshape.70 = f32[40,8,32]{2,1,0:T(8,128)S(1)} reshape(f32[40,256]{1,0:T(8,128)} %get-tuple-element.5) | data formatting | bytes 81920 | tf_op jit(solution)/shard_map/reshape | solution.py:157
  45.1 0.4 slice_reduce_fusion
  45.4 1.3 %dynamic_slice.3 = s32[1,1]{0,1:T(1,128)} dynamic-slice(s32[32,16]{0,1:T(8,128)} %param.12, s32[]{:T(128)S(6)} %select_n.33, s32[]{:T(128)S(6)} %select_n.34), dynamic_slice_sizes={1,1} | dynamic-slice | bytes 12 | tf_op jit(solution)/shard_map/dynamic_slice | solution.py:182
  46.7 0.6 iota_compare_fusion.3
  47.4 0.7 bitcast_select_fusion
  48.1 1.4 %fusion.12 = (f32[40]{0:T(128)S(1)}, bf16[1,1,40]{2,1,0:T(2,128)(2,1)}) fusion(s32[]{:T(128)} %bitcast, f32[32]{0:T(128)S(1)} %copy-done.7, f32[40,32]{1,0:T(8,128)S(1)} %reduce_sum.27, f32[40]{0:T(128)S(1)} %slice_reduce_fusion), kind=kOutput, calls=%fused_computation.26 | convolution fusion | flops 16920 | bytes 5652 | tf_op jit(solution)/shard_map/dot_general | solution.py:159
  49.9 14.6 %all_to_all.5 = f32[16,8,128]{2,1,0:T(8,128)S(1)} all-to-all(f32[16,8,128]{2,1,0:T(8,128)S(1)} %convolution_bitcast_fusion), channel_id=1, replica_groups=mesh['bulk'=32,'seg'=16] {'seg'}, dimensions={0} | all-to-all | bytes 131072 | tf_op jit(solution)/shard_map/all_to_all | solution.py:196
  64.5 0.6 reduce_sum.29
  (23 shorter events, 0.5 us)
Async XLA Ops:
  0.6 48.9 %copy-start = (bf16[32,128]{1,0:T(8,128)(2,1)S(1)}, bf16[32,128]{1,0:T(8,128)(2,1)}, u32[]{:S(2)}) copy-start(bf16[32,128]{1,0:T(8,128)(2,1)} %param.18) | copy-start | bytes 24580
  9.4 3.6 %copy-start.5 = (s32[3]{0:T(128)S(1)}, s32[3]{0:T(128)}, u32[]{:S(2)}) copy-start(s32[3]{0:T(128)} %constant.36) | copy-start | bytes 40
  9.4 3.6 %copy-start.4 = (bf16[32,24]{0,1:T(8,128)(2,1)S(1)}, bf16[32,24]{0,1:T(8,128)(2,1)}, u32[]{:S(2)}) copy-start(bf16[32,24]{0,1:T(8,128)(2,1)} %param.14) | copy-start | bytes 4612
  10.6 7.0 %copy-start.1 = (bf16[40,1,8,1,8,32]{5,4,3,2,0,1:T(8,128)(2,1)S(1)}, bf16[40,1,8,1,8,32]{5,4,3,2,0,1:T(8,128)(2,1)}, u32[]{:S(2)}) copy-start(bf16[40,1,8,1,8,32]{5,4,3,2,0,1:T(8,128)(2,1)} %get-tuple-element.7) | copy-start | bytes 491524
  10.6 7.0 %copy-start.2 = (bf16[40,1,8,1,8,32]{5,4,3,2,0,1:T(8,128)(2,1)S(1)}, bf16[40,1,8,1,8,32]{5,4,3,2,0,1:T(8,128)(2,1)}, u32[]{:S(2)}) copy-start(bf16[40,1,8,1,8,32]{5,4,3,2,0,1:T(8,128)(2,1)} %get-tuple-element.8) | copy-start | bytes 491524
  10.6 7.0 %copy-start.3 = (bf16[40,1,8,1,8,32]{5,4,3,2,0,1:T(8,128)(2,1)S(1)}, bf16[40,1,8,1,8,32]{5,4,3,2,0,1:T(8,128)(2,1)}, u32[]{:S(2)}) copy-start(bf16[40,1,8,1,8,32]{5,4,3,2,0,1:T(8,128)(2,1)} %get-tuple-element.9) | copy-start | bytes 491524
  22.2 25.2 %copy-start.6 = (s32[1,1,40]{2,1,0:T(1,128)S(1)}, s32[1,1,40]{2,1,0:T(1,128)}, u32[]{:S(2)}) copy-start(s32[1,1,40]{2,1,0:T(1,128)} %param.13) | copy-start | bytes 484
  22.2 25.9 %copy-start.7 = (f32[32]{0:T(128)S(1)}, f32[32]{0:T(128)}, u32[]{:S(2)}) copy-start(f32[32]{0:T(128)} %param.17) | copy-start | bytes 388

commit v7 on v6

--- a/solution.py
+++ b/solution.py
@@ -13,7 +13,8 @@
 
 
 def conv_kernel(
-    x_ref, q_ref, first_bias_ref, w_ref, b_ref, pool_ref, weight_ref, pad_ref, col_ref, band_ref
+    x_ref, q_ref, first_bias_ref, w_ref, b_ref, pool_ref, weight_ref, pad_ref, col_ref, band_ref,
+    tiled_ref,
 ):
     rows, lanes = pad_ref.shape[0] - 2 * PAD_ROWS, pad_ref.shape[1]
     side = CS // 2
@@ -26,16 +27,14 @@
         in_row = lax.broadcasted_iota(jnp.int32, (channels, lanes), 0)
         spread = (out_lane % channels == in_row).astype(jnp.bfloat16)
         z_lane = out_lane // channels
+        all_taps = w_ref[...].reshape(LAYERS * 27 * channels, channels)
+        tiled_ref[...] = jnp.dot(all_taps, spread, preferred_element_type=jnp.float32)
         for layer_index in range(LAYERS):
             for tap in range(9):
-                tiled = [
-                    jnp.dot(
-                        w_ref[layer_index, tap * 3 + shift_c],
-                        spread,
-                        preferred_element_type=jnp.float32,
-                    )
-                    for shift_c in range(3)
-                ]
+                tiled = []
+                for shift_c in range(3):
+                    first_row = ((layer_index * 9 + tap) * 3 + shift_c) * channels
+                    tiled.append(tiled_ref[first_row:first_row + channels, :])
                 for z_in in range(side):
                     block = jnp.where(
                         z_lane == z_in + 1,
@@ -128,6 +127,7 @@
             pltpu.VMEM((block_rows + 2 * PAD_ROWS, lanes), jnp.float32),
             pltpu.VMEM((block_rows, 9 * lanes), jnp.bfloat16),
             pltpu.VMEM((LAYERS, 9 * lanes, lanes), jnp.bfloat16),
+            pltpu.VMEM((LAYERS * 27 * channels, lanes), jnp.float32),
         ],
         compiler_params=pltpu.CompilerParams(dimension_semantics=("arbitrary",)),
     )(features, patch_matrix, first_bias, taps, bias)

time: 65.7 us -> 65.5 us (level)
  no operation moved by 1% of the time
where the time goes in v7:
time: 65.5 us; the launch traced here: 64.9 us
  local copies, waits for them, and re-layouts  23.6 us (36%)
  Pallas kernels  20.9 us (32%)
  blocking collectives  14.6 us (22%)
  other arithmetic  3.2 us (5%)
  matrix products  1.76 us (3%)
  between operations  0.77 us (1%)
    pallas_call x1, Pallas kernels, conv_layers(): pl.pallas_call(conv_kernel, grid=(total_rows // block_rows,), in_specs=[p...  20.9 us
    all_to_all x1, blocking collectives, per_device(): arrived = lax.all_to_all(partial_value, 'seg', 0, 0, tiled=True)  14.6 us
    concatenate x1, local copies, waits for them, and re-layouts, run_network(): jnp.concatenate([cells[:, channel, :, half].reshape(rows_here * side_half...  4.46 us
    concatenate x2, local copies, waits for them, and re-layouts, run_network(): stacked = jnp.concatenate([mask_rows, em_rows[:, None, :]], axis=1)  4.12 us
    unnamed x18, local copies, waits for them, and re-layouts  3.84 us
    slice x2, local copies, waits for them, and re-layouts, run_network(): cells[:, channel, :, half]  2.99 us
    select_n x1, local copies, waits for them, and re-layouts, conv_layers(): jnp.where(z_in == z_out, per_cell[:, :, :, None, :, None, :], 0)  1.94 us
    dot_general x1, matrix products, run_network(): logits = jnp.dot(pooled, score_weight, precision=highest)  1.4 us

profile of v7, /device:TPU:2, one launch (start us, length us, event | category | flops | bytes accessed | tf_op | source)
XLA Modules:
  0.0 64.9 jit_solution(3804106460614910315)
XLA Ops:
  0.7 0.7 %slice.40 = f32[3,32]{1,0:T(4,128)S(1)} slice(f32[4,32]{1,0:T(4,128)} %param.16), slice={[1:4], [0:32]} | slice | bytes 768 | tf_op jit(solution)/shard_map/slice | solution.py:106
  1.3 0.7 %slice_bitcast_fusion = f32[32]{0:T(128)S(1)} fusion(f32[4,32]{1,0:T(4,128)} %param.16), kind=kLoop, calls=%fused_computation.22 | loop fusion | bytes 256 | tf_op jit(solution)/shard_map/tile | solution.py:104
  2.0 1.5 %copy.19 = bf16[1,1,40,2,4096]{4,2,3,1,0:T(8,128)(2,1)S(1)} copy(bf16[1,1,40,2,4096]{4,3,2,1,0:T(2,128)(2,1)} %param.11) | data formatting | bytes 1310720 | tf_op args[1]
  3.5 2.1 %concatenate.9 = bf16[40,2,8,2,8,32]{5,4,3,2,0,1:T(8,128)(2,1)S(1)} reshape(bf16[1,1,40,2,4096]{4,2,3,1,0:T(8,128)(2,1)S(1)} %copy.19) | data formatting | bytes 1310720 | tf_op jit(solution)/shard_map/concatenate | solution.py:145
  5.6 1.8 %fusion.10 = (bf16[40,1,8,1,8,32]{5,4,3,2,0,1:T(8,128)(2,1)S(1)}, bf16[40,1,8,1,8,32]{5,4,3,2,0,1:T(8,128)(2,1)}, bf16[40,1,8,1,8,32]{5,4,3,2,0,1:T(8,128)(2,1)}, bf16[40,1,8,1,8,32]{5,4,3,2,0,1:T(8,128)(2,1)}) fusion(bf16[40,2,8,2,8,32]{5,4,3,2,0,1:T(8,128)(2,1)S(1)} %concatenate.9), kind=kLoop, calls=%fused_computation.24 | loop fusion | bytes 1310720 | tf_op jit(solution)/shard_map/slice | solution.py:149
  7.3 2.0 %concatenate.10 = bf16[40,1,8,2,8,32]{5,4,3,2,0,1:T(8,128)(2,1)S(1)} reshape(bf16[1,1,40,4096]{3,2,1,0:T(8,128)(2,1)} %param.10) | data formatting | bytes 655360 | tf_op jit(solution)/shard_map/concatenate | solution.py:145
  9.4 1.2 %fusion.11 = (bf16[40,1,8,1,8,32]{5,4,3,2,0,1:T(8,128)(2,1)S(1)}, bf16[40,1,8,1,8,32]{5,4,3,2,0,1:T(8,128)(2,1)}) fusion(bf16[40,1,8,2,8,32]{5,4,3,2,0,1:T(8,128)(2,1)S(1)} %concatenate.10), kind=kLoop, calls=%fused_computation.25 | loop fusion | bytes 655360 | tf_op jit(solution)/shard_map/slice | solution.py:149
  10.6 2.4 %copy.20 = bf16[3,27,32,32]{2,3,1,0:T(8,128)(2,1)} copy(bf16[3,27,32,32]{3,2,1,0:T(8,128)(2,1)} %param.15) | data formatting | bytes 331776 | tf_op args[5]
  13.0 0.6 gather_fusion
  13.6 0.9 %broadcast_select_fusion = bf16[3,2,2,8,2,8,32]{6,5,4,3,2,1,0:T(8,128)(2,1)} fusion(pred[8,8]{1,0:T(8,128)(4,1)S(1)} %iota_compare_fusion.2, bf16[3,2,2,2,32]{4,3,2,1,0:T(2,128)(2,1)S(1)} %gather_fusion), kind=kLoop, calls=%fused_computation.12 | loop fusion | flops 49152 | bytes 99904 | tf_op jit(solution)/shard_map/jit(_where)/select_n | solution.py:101
  14.4 1.9 %select_n.37.q_ref = bf16[192,256]{1,0:T(8,128)(2,1)} reshape(bf16[3,2,2,8,2,8,32]{6,5,4,3,2,1,0:T(8,128)(2,1)} %broadcast_select_fusion) | data formatting | bytes 196608 | tf_op jit(solution)/shard_map/jit(_where)/select_n | solution.py:101
  16.4 0.7 %tile.18.b_ref = f32[3,1,256]{2,1,0:T(1,128)} reshape(f32[3,8,32]{2,1,0:T(8,128)S(1)} %tile.17) | data formatting | bytes 6144 | tf_op jit(solution)/shard_map/tile | solution.py:106
  17.1 0.6 reshape_tile.4.first_bias_ref
  17.7 4.5 %concatenate.11.x_ref = bf16[2560,192]{1,0:T(8,128)(2,1)} concatenate(bf16[2560,32]{1,0:T(8,128)(2,1)S(1)} %bitcast.52, bf16[2560,32]{1,0:T(8,128)(2,1)S(1)} %bitcast.51, bf16[2560,32]{1,0:T(8,128)(2,1)S(1)} %bitcast.50, bf16[2560,32]{1,0:T(8,128)(2,1)S(1)} %bitcast.49, bf16[2560,32]{1,0:T(8,128)(2,1)} %bitcast.54, bf16[2560,32]{1,0:T(8,128)(2,1)S(1)} %bitcast.53), dimensions={1} | concatenate | bytes 1966080 | tf_op jit(solution)/shard_map/concatenate | solution.py:147
  22.2 20.9 %shard_map.113 = (f32[40,256]{1,0:T(8,128)}, f32[40,256]{1,0:T(8,128)}) custom-call(bf16[2560,192]{1,0:T(8,128)(2,1)} %concatenate.11.x_ref, bf16[192,256]{1,0:T(8,128)(2,1)} %select_n.37.q_ref, f32[1,256]{1,0:T(1,128)} %reshape_tile.4.first_bias_ref, bf16[3,27,32,32]{3,2,1,0:T(8,128)(2,1)} %bitcast.48, f32[3,1,256]{2,1,0:T(1,128)} %tile.18.b_ref), custom_call_target="tpu_custom_call" | custom-call | tf_op jit(solution)/shard_map/pallas_call | solution.py:108
  43.1 0.9 %reshape.69 = f32[40,8,32]{2,1,0:T(8,128)S(1)} reshape(f32[40,256]{1,0:T(8,128)} %get-tuple-element.4) | data formatting | bytes 81920 | tf_op jit(solution)/shard_map/reshape | solution.py:156
  44.0 0.9 %reshape.70 = f32[40,8,32]{2,1,0:T(8,128)S(1)} reshape(f32[40,256]{1,0:T(8,128)} %get-tuple-element.5) | data formatting | bytes 81920 | tf_op jit(solution)/shard_map/reshape | solution.py:157
  44.8 0.4 slice_reduce_fusion
  45.2 1.3 %dynamic_slice.3 = s32[1,1]{0,1:T(1,128)} dynamic-slice(s32[32,16]{0,1:T(8,128)} %param.12, s32[]{:T(128)S(6)} %select_n.33, s32[]{:T(128)S(6)} %select_n.34), dynamic_slice_sizes={1,1} | dynamic-slice | bytes 12 | tf_op jit(solution)/shard_map/dynamic_slice | solution.py:182
  46.5 0.6 iota_compare_fusion.3
  47.1 0.7 %bitcast_select_fusion = s32[40]{0:T(128)S(1)} fusion(s32[1,1,40]{2,1,0:T(1,128)S(1)} %copy-done.6, s32[]{:T(128)} %bitcast), kind=kLoop, calls=%fused_computation.19 | loop fusion | flops 80 | bytes 324 | tf_op jit(solution)/shard_map/jit(_where)/select_n | solution.py:191
  47.9 1.4 %fusion.12 = (f32[40]{0:T(128)S(1)}, bf16[1,1,40]{2,1,0:T(2,128)(2,1)}) fusion(s32[]{:T(128)} %bitcast, f32[32]{0:T(128)S(1)} %copy-done.7, f32[40,32]{1,0:T(8,128)S(1)} %reduce_sum.27, f32[40]{0:T(128)S(1)} %slice_reduce_fusion), kind=kOutput, calls=%fused_computation.26 | convolution fusion | flops 16920 | bytes 5652 | tf_op jit(solution)/shard_map/dot_general | solution.py:159
  49.6 14.6 %all_to_all.5 = f32[16,8,128]{2,1,0:T(8,128)S(1)} all-to-all(f32[16,8,128]{2,1,0:T(8,128)S(1)} %convolution_bitcast_fusion), channel_id=1, replica_groups=mesh['bulk'=32,'seg'=16] {'seg'}, dimensions={0} | all-to-all | bytes 131072 | tf_op jit(solution)/shard_map/all_to_all | solution.py:196
  64.3 0.6 reduce_sum.29
  (23 shorter events, 0.5 us)
Async XLA Ops:
  0.6 48.6 %copy-start = (bf16[32,128]{1,0:T(8,128)(2,1)S(1)}, bf16[32,128]{1,0:T(8,128)(2,1)}, u32[]{:S(2)}) copy-start(bf16[32,128]{1,0:T(8,128)(2,1)} %param.18) | copy-start | bytes 24580
  9.4 3.6 %copy-start.5 = (s32[3]{0:T(128)S(1)}, s32[3]{0:T(128)}, u32[]{:S(2)}) copy-start(s32[3]{0:T(128)} %constant.36) | copy-start | bytes 40
  9.4 3.6 %copy-start.4 = (bf16[32,24]{0,1:T(8,128)(2,1)S(1)}, bf16[32,24]{0,1:T(8,128)(2,1)}, u32[]{:S(2)}) copy-start(bf16[32,24]{0,1:T(8,128)(2,1)} %param.14) | copy-start | bytes 4612
  10.6 7.0 %copy-start.1 = (bf16[40,1,8,1,8,32]{5,4,3,2,0,1:T(8,128)(2,1)S(1)}, bf16[40,1,8,1,8,32]{5,4,3,2,0,1:T(8,128)(2,1)}, u32[]{:S(2)}) copy-start(bf16[40,1,8,1,8,32]{5,4,3,2,0,1:T(8,128)(2,1)} %get-tuple-element.7) | copy-start | bytes 491524
  10.6 7.0 %copy-start.2 = (bf16[40,1,8,1,8,32]{5,4,3,2,0,1:T(8,128)(2,1)S(1)}, bf16[40,1,8,1,8,32]{5,4,3,2,0,1:T(8,128)(2,1)}, u32[]{:S(2)}) copy-start(bf16[40,1,8,1,8,32]{5,4,3,2,0,1:T(8,128)(2,1)} %get-tuple-element.8) | copy-start | bytes 491524
  10.6 7.0 %copy-start.3 = (bf16[40,1,8,1,8,32]{5,4,3,2,0,1:T(8,128)(2,1)S(1)}, bf16[40,1,8,1,8,32]{5,4,3,2,0,1:T(8,128)(2,1)}, u32[]{:S(2)}) copy-start(bf16[40,1,8,1,8,32]{5,4,3,2,0,1:T(8,128)(2,1)} %get-tuple-element.9) | copy-start | bytes 491524
  22.2 25.0 %copy-start.6 = (s32[1,1,40]{2,1,0:T(1,128)S(1)}, s32[1,1,40]{2,1,0:T(1,128)}, u32[]{:S(2)}) copy-start(s32[1,1,40]{2,1,0:T(1,128)} %param.13) | copy-start | bytes 484
  22.2 25.7 %copy-start.7 = (f32[32]{0:T(128)S(1)}, f32[32]{0:T(128)}, u32[]{:S(2)}) copy-start(f32[32]{0:T(128)} %param.17) | copy-start | bytes 388

commit v8 on v7

--- a/solution.py
+++ b/solution.py
@@ -8,7 +8,7 @@
 CS = 16
 LAYERS = 3
 SEG_DEV = 8
-BLOCK_PAIRS = 8
+BLOCK_PAIRS = 40
 PAD_ROWS = 16
 
 

time: 65.5 us -> 65.9 us (level)
  no operation moved by 1% of the time
where the time goes in v8:
time: 65.9 us; the launch traced here: 65.2 us
  local copies, waits for them, and re-layouts  23.6 us (36%)
  Pallas kernels  21.3 us (32%)
  blocking collectives  14.6 us (22%)
  other arithmetic  3.2 us (5%)
  matrix products  1.76 us (3%)
  between operations  0.77 us (1%)
    pallas_call x1, Pallas kernels, conv_layers(): pl.pallas_call(conv_kernel, grid=(total_rows // block_rows,), in_specs=[p...  21.3 us
    all_to_all x1, blocking collectives, per_device(): arrived = lax.all_to_all(partial_value, 'seg', 0, 0, tiled=True)  14.6 us
    concatenate x1, local copies, waits for them, and re-layouts, run_network(): jnp.concatenate([cells[:, channel, :, half].reshape(rows_here * side_half...  4.46 us
    concatenate x2, local copies, waits for them, and re-layouts, run_network(): stacked = jnp.concatenate([mask_rows, em_rows[:, None, :]], axis=1)  4.12 us
    unnamed x18, local copies, waits for them, and re-layouts  3.84 us
    slice x2, local copies, waits for them, and re-layouts, run_network(): cells[:, channel, :, half]  2.99 us
    select_n x1, local copies, waits for them, and re-layouts, conv_layers(): jnp.where(z_in == z_out, per_cell[:, :, :, None, :, None, :], 0)  1.94 us
    dot_general x1, matrix products, run_network(): logits = jnp.dot(pooled, score_weight, precision=highest)  1.4 us

profile of v8, /device:TPU:2, one launch (start us, length us, event | category | flops | bytes accessed | tf_op | source)
XLA Modules:
  0.0 65.2 jit_solution(15163548276734422149)
XLA Ops:
  0.7 0.7 %slice.40 = f32[3,32]{1,0:T(4,128)S(1)} slice(f32[4,32]{1,0:T(4,128)} %param.16), slice={[1:4], [0:32]} | slice | bytes 768 | tf_op jit(solution)/shard_map/slice | solution.py:106
  1.3 0.7 %slice_bitcast_fusion = f32[32]{0:T(128)S(1)} fusion(f32[4,32]{1,0:T(4,128)} %param.16), kind=kLoop, calls=%fused_computation.22 | loop fusion | bytes 256 | tf_op jit(solution)/shard_map/tile | solution.py:104
  2.0 1.5 %copy.19 = bf16[1,1,40,2,4096]{4,2,3,1,0:T(8,128)(2,1)S(1)} copy(bf16[1,1,40,2,4096]{4,3,2,1,0:T(2,128)(2,1)} %param.11) | data formatting | bytes 1310720 | tf_op args[1]
  3.5 2.1 %concatenate.9 = bf16[40,2,8,2,8,32]{5,4,3,2,0,1:T(8,128)(2,1)S(1)} reshape(bf16[1,1,40,2,4096]{4,2,3,1,0:T(8,128)(2,1)S(1)} %copy.19) | data formatting | bytes 1310720 | tf_op jit(solution)/shard_map/concatenate | solution.py:145
  5.6 1.8 %fusion.10 = (bf16[40,1,8,1,8,32]{5,4,3,2,0,1:T(8,128)(2,1)S(1)}, bf16[40,1,8,1,8,32]{5,4,3,2,0,1:T(8,128)(2,1)}, bf16[40,1,8,1,8,32]{5,4,3,2,0,1:T(8,128)(2,1)}, bf16[40,1,8,1,8,32]{5,4,3,2,0,1:T(8,128)(2,1)}) fusion(bf16[40,2,8,2,8,32]{5,4,3,2,0,1:T(8,128)(2,1)S(1)} %concatenate.9), kind=kLoop, calls=%fused_computation.24 | loop fusion | bytes 1310720 | tf_op jit(solution)/shard_map/slice | solution.py:149
  7.3 2.0 %concatenate.10 = bf16[40,1,8,2,8,32]{5,4,3,2,0,1:T(8,128)(2,1)S(1)} reshape(bf16[1,1,40,4096]{3,2,1,0:T(8,128)(2,1)} %param.10) | data formatting | bytes 655360 | tf_op jit(solution)/shard_map/concatenate | solution.py:145
  9.4 1.2 %fusion.11 = (bf16[40,1,8,1,8,32]{5,4,3,2,0,1:T(8,128)(2,1)S(1)}, bf16[40,1,8,1,8,32]{5,4,3,2,0,1:T(8,128)(2,1)}) fusion(bf16[40,1,8,2,8,32]{5,4,3,2,0,1:T(8,128)(2,1)S(1)} %concatenate.10), kind=kLoop, calls=%fused_computation.25 | loop fusion | bytes 655360 | tf_op jit(solution)/shard_map/slice | solution.py:149
  10.6 2.4 %copy.20 = bf16[3,27,32,32]{2,3,1,0:T(8,128)(2,1)} copy(bf16[3,27,32,32]{3,2,1,0:T(8,128)(2,1)} %param.15) | data formatting | bytes 331776 | tf_op args[5]
  13.0 0.6 gather_fusion
  13.6 0.9 %broadcast_select_fusion = bf16[3,2,2,8,2,8,32]{6,5,4,3,2,1,0:T(8,128)(2,1)} fusion(pred[8,8]{1,0:T(8,128)(4,1)S(1)} %iota_compare_fusion.2, bf16[3,2,2,2,32]{4,3,2,1,0:T(2,128)(2,1)S(1)} %gather_fusion), kind=kLoop, calls=%fused_computation.12 | loop fusion | flops 49152 | bytes 99904 | tf_op jit(solution)/shard_map/jit(_where)/select_n | solution.py:101
  14.4 1.9 %select_n.37.q_ref = bf16[192,256]{1,0:T(8,128)(2,1)} reshape(bf16[3,2,2,8,2,8,32]{6,5,4,3,2,1,0:T(8,128)(2,1)} %broadcast_select_fusion) | data formatting | bytes 196608 | tf_op jit(solution)/shard_map/jit(_where)/select_n | solution.py:101
  16.4 0.7 %tile.18.b_ref = f32[3,1,256]{2,1,0:T(1,128)} reshape(f32[3,8,32]{2,1,0:T(8,128)S(1)} %tile.17) | data formatting | bytes 6144 | tf_op jit(solution)/shard_map/tile | solution.py:106
  17.1 0.6 reshape_tile.4.first_bias_ref
  17.7 4.5 %concatenate.11.x_ref = bf16[2560,192]{1,0:T(8,128)(2,1)} concatenate(bf16[2560,32]{1,0:T(8,128)(2,1)S(1)} %bitcast.52, bf16[2560,32]{1,0:T(8,128)(2,1)S(1)} %bitcast.51, bf16[2560,32]{1,0:T(8,128)(2,1)S(1)} %bitcast.50, bf16[2560,32]{1,0:T(8,128)(2,1)S(1)} %bitcast.49, bf16[2560,32]{1,0:T(8,128)(2,1)} %bitcast.54, bf16[2560,32]{1,0:T(8,128)(2,1)S(1)} %bitcast.53), dimensions={1} | concatenate | bytes 1966080 | tf_op jit(solution)/shard_map/concatenate | solution.py:147
  22.2 21.3 %shard_map.113 = (f32[40,256]{1,0:T(8,128)}, f32[40,256]{1,0:T(8,128)}) custom-call(bf16[2560,192]{1,0:T(8,128)(2,1)} %concatenate.11.x_ref, bf16[192,256]{1,0:T(8,128)(2,1)} %select_n.37.q_ref, f32[1,256]{1,0:T(1,128)} %reshape_tile.4.first_bias_ref, bf16[3,27,32,32]{3,2,1,0:T(8,128)(2,1)} %bitcast.48, f32[3,1,256]{2,1,0:T(1,128)} %tile.18.b_ref), custom_call_target="tpu_custom_call" | custom-call | tf_op jit(solution)/shard_map/pallas_call | solution.py:108
  43.4 0.9 %reshape.69 = f32[40,8,32]{2,1,0:T(8,128)S(1)} reshape(f32[40,256]{1,0:T(8,128)} %get-tuple-element.4) | data formatting | bytes 81920 | tf_op jit(solution)/shard_map/reshape | solution.py:156
  44.3 0.9 %reshape.70 = f32[40,8,32]{2,1,0:T(8,128)S(1)} reshape(f32[40,256]{1,0:T(8,128)} %get-tuple-element.5) | data formatting | bytes 81920 | tf_op jit(solution)/shard_map/reshape | solution.py:157
  45.2 0.4 slice_reduce_fusion
  45.6 1.3 %dynamic_slice.3 = s32[1,1]{0,1:T(1,128)} dynamic-slice(s32[32,16]{0,1:T(8,128)} %param.12, s32[]{:T(128)S(6)} %select_n.33, s32[]{:T(128)S(6)} %select_n.34), dynamic_slice_sizes={1,1} | dynamic-slice | bytes 12 | tf_op jit(solution)/shard_map/dynamic_slice | solution.py:182
  46.8 0.6 iota_compare_fusion.3
  47.5 0.7 bitcast_select_fusion
  48.2 1.4 %fusion.12 = (f32[40]{0:T(128)S(1)}, bf16[1,1,40]{2,1,0:T(2,128)(2,1)}) fusion(s32[]{:T(128)} %bitcast, f32[32]{0:T(128)S(1)} %copy-done.7, f32[40,32]{1,0:T(8,128)S(1)} %reduce_sum.27, f32[40]{0:T(128)S(1)} %slice_reduce_fusion), kind=kOutput, calls=%fused_computation.26 | convolution fusion | flops 16920 | bytes 5652 | tf_op jit(solution)/shard_map/dot_general | solution.py:159
  50.0 14.6 %all_to_all.5 = f32[16,8,128]{2,1,0:T(8,128)S(1)} all-to-all(f32[16,8,128]{2,1,0:T(8,128)S(1)} %convolution_bitcast_fusion), channel_id=1, replica_groups=mesh['bulk'=32,'seg'=16] {'seg'}, dimensions={0} | all-to-all | bytes 131072 | tf_op jit(solution)/shard_map/all_to_all | solution.py:196
  64.6 0.6 reduce_sum.29
  (23 shorter events, 0.5 us)
Async XLA Ops:
  0.6 49.0 %copy-start = (bf16[32,128]{1,0:T(8,128)(2,1)S(1)}, bf16[32,128]{1,0:T(8,128)(2,1)}, u32[]{:S(2)}) copy-start(bf16[32,128]{1,0:T(8,128)(2,1)} %param.18) | copy-start | bytes 24580
  9.4 3.6 %copy-start.5 = (s32[3]{0:T(128)S(1)}, s32[3]{0:T(128)}, u32[]{:S(2)}) copy-start(s32[3]{0:T(128)} %constant.36) | copy-start | bytes 40
  9.4 3.6 %copy-start.4 = (bf16[32,24]{0,1:T(8,128)(2,1)S(1)}, bf16[32,24]{0,1:T(8,128)(2,1)}, u32[]{:S(2)}) copy-start(bf16[32,24]{0,1:T(8,128)(2,1)} %param.14) | copy-start | bytes 4612
  10.6 7.0 %copy-start.1 = (bf16[40,1,8,1,8,32]{5,4,3,2,0,1:T(8,128)(2,1)S(1)}, bf16[40,1,8,1,8,32]{5,4,3,2,0,1:T(8,128)(2,1)}, u32[]{:S(2)}) copy-start(bf16[40,1,8,1,8,32]{5,4,3,2,0,1:T(8,128)(2,1)} %get-tuple-element.7) | copy-start | bytes 491524
  10.6 7.0 %copy-start.2 = (bf16[40,1,8,1,8,32]{5,4,3,2,0,1:T(8,128)(2,1)S(1)}, bf16[40,1,8,1,8,32]{5,4,3,2,0,1:T(8,128)(2,1)}, u32[]{:S(2)}) copy-start(bf16[40,1,8,1,8,32]{5,4,3,2,0,1:T(8,128)(2,1)} %get-tuple-element.8) | copy-start | bytes 491524
  10.6 7.0 %copy-start.3 = (bf16[40,1,8,1,8,32]{5,4,3,2,0,1:T(8,128)(2,1)S(1)}, bf16[40,1,8,1,8,32]{5,4,3,2,0,1:T(8,128)(2,1)}, u32[]{:S(2)}) copy-start(bf16[40,1,8,1,8,32]{5,4,3,2,0,1:T(8,128)(2,1)} %get-tuple-element.9) | copy-start | bytes 491524
  22.2 25.3 %copy-start.6 = (s32[1,1,40]{2,1,0:T(1,128)S(1)}, s32[1,1,40]{2,1,0:T(1,128)}, u32[]{:S(2)}) copy-start(s32[1,1,40]{2,1,0:T(1,128)} %param.13) | copy-start | bytes 484
  22.2 26.0 %copy-start.7 = (f32[32]{0:T(128)S(1)}, f32[32]{0:T(128)}, u32[]{:S(2)}) copy-start(f32[32]{0:T(128)} %param.17) | copy-start | bytes 388
